TPU v7x, 32 devices: a whole 2x2x4 slice. The times are simulated.
32 devices in a mesh: rows: 8 (over z, y), cols: 4 (over x, core).
Axes of the slice: x: 2, y: 2, z: 4, core: 2. Of those that a mesh axis runs over, the one named last changes fastest.
Arguments:
- snapshots: float32 [512, 65536], P(('cols', 'rows'))
- pair_table: int32 [4], replicated, may hold values from 0 to 3, as said below
Outputs:
- rotated: float32 [512, 65536], P('cols', 'rows')
Inputs may be any that keep to these rules, and one draw needn't show every extreme that they name: pair_table[c] = c XOR m for one m shared by all c, m a power of two below 4, so blocks are paired two by two along one binary digit.
All inputs are finite; a program needn't handle non-finite values.
Results may differ from a plain program's by a relative error of at most 0.0003.
Values sent between devices are 32-bit elements; how exact they have to be, the bound alone decides.
No kernel may reach another device: no remote copies, remote signals or barrier semaphores. Data moves between devices by JAX's collectives and lax.ppermute only.
A program may use at most 64 MiB of HBM per device.

v0:
```python
import functools

import jax
import jax.numpy as jnp
import numpy as np
from jax import lax
from jax.experimental import pallas as pl
from jax.experimental.pallas import tpu as pltpu
from jax.sharding import PartitionSpec as P

ROUNDS = 8


def partner_2(value, axis, bit):
    mask = 2**bit
    pairs = [(source, source ^ mask) for source in range(lax.axis_size(axis))]
    return lax.ppermute(value, axis, pairs)


def jacobi_kernel(gram_ref, rotation_ref):
    highest = lax.Precision.HIGHEST
    order_dim = gram_ref.shape[0]
    last_idx = order_dim - 1
    width = order_dim // 2
    gram = gram_ref[...]
    row_col = lax.broadcasted_iota(jnp.int32, (order_dim, 1), 0)
    row_full = lax.broadcasted_iota(jnp.int32, (order_dim, order_dim), 0)
    col_full = lax.broadcasted_iota(jnp.int32, (order_dim, order_dim), 1)
    eye = row_full == col_full
    rotation = None
    for round_idx in range(ROUNDS):
        fixed = round_idx % last_idx
        mirror = 2 * fixed - row_col
        mirror = jnp.where(mirror < 0, mirror + last_idx, mirror)
        partner = jnp.where(row_col == fixed, last_idx, jnp.where(row_col == last_idx, fixed, mirror))
        offset = row_col - fixed
        offset = jnp.where(offset < 0, offset + last_idx, offset)
        is_first = (row_col == last_idx) | ((row_col != fixed) & (offset >= 1) & (offset <= width - 1))
        swap = (col_full == partner).astype(jnp.float32)
        on_diag = jnp.where(eye, gram, 0.0)
        diag_own = jnp.sum(on_diag, axis=1, keepdims=True)
        diag_row = jnp.sum(on_diag, axis=0, keepdims=True)
        diag_mate = jnp.sum(swap * diag_row, axis=1, keepdims=True)
        picked = gram * swap
        cross_second = jnp.sum(picked, axis=1, keepdims=True)
        cross_row = jnp.sum(picked, axis=0, keepdims=True)
        cross_first = jnp.sum(jnp.where(eye, cross_row, 0.0), axis=1, keepdims=True)
        cross_val = jnp.where(is_first, cross_first, cross_second)
        spread = jnp.where(is_first, diag_mate - diag_own, diag_own - diag_mate)
        hypot_val = jnp.sqrt(spread * spread + 4.0 * cross_val * cross_val)
        denom = jnp.sqrt(2.0 * hypot_val * (hypot_val + jnp.abs(spread)))
        sign_val = jnp.where(spread >= 0.0, 1.0, -1.0)
        cosine = (hypot_val + jnp.abs(spread)) / denom
        sine_val = 2.0 * cross_val * sign_val / denom
        signed = jnp.where(is_first, sine_val, -sine_val)
        diag_part = jnp.where(eye, cosine, 0.0)
        turn = diag_part + swap * signed
        turn_t = diag_part - swap * signed
        gram = jnp.dot(
            turn_t,
            jnp.dot(gram, turn, precision=highest, preferred_element_type=jnp.float32),
            precision=highest,
            preferred_element_type=jnp.float32,
        )
        rotation = turn if rotation is None else jnp.dot(
            rotation, turn, precision=highest, preferred_element_type=jnp.float32
        )
    rotation_ref[...] = rotation

def jacobi_pallas(gram):
    return pl.pallas_call(
        jacobi_kernel,
        out_shape=jax.ShapeDtypeStruct(gram.shape, jnp.float32),
        in_specs=[pl.BlockSpec(memory_space=pltpu.VMEM)],
        out_specs=pl.BlockSpec(memory_space=pltpu.VMEM),
    )(gram)


def gram_kernel(mine_ref, theirs_ref, out_ref, acc_ref):
    step = pl.program_id(0)

    @pl.when(step == 0)
    def _():
        acc_ref[...] = jnp.zeros_like(acc_ref)

    stacked = jnp.concatenate([mine_ref[...], theirs_ref[...]], 0)
    acc_ref[...] += lax.dot_general(
        stacked,
        stacked,
        (((1,), (1,)), ((), ())),
        precision=lax.Precision.HIGHEST,
        preferred_element_type=jnp.float32,
    )

    @pl.when(step == pl.num_programs(0) - 1)
    def _():
        width = mine_ref.shape[0]
        row = lax.broadcasted_iota(jnp.int32, (width, width), 0)
        col = lax.broadcasted_iota(jnp.int32, (width, width), 1)
        gram_theirs = acc_ref[width:, width:]
        out_ref[:width, :] = jnp.where(row <= col, acc_ref[:width, :width], gram_theirs)
        out_ref[width : 2 * width, :] = acc_ref[:width, width:]
        diag_theirs = jnp.sum(jnp.where(row == col, gram_theirs, 0.0), axis=0, keepdims=True)
        out_ref[2 * width :, :] = jnp.broadcast_to(diag_theirs, (8, width))


def gram_store_kernel(mine_ref, theirs_ref, own_in, other_in, out_ref, own_ref, other_ref, acc_ref):
    del own_in, other_in
    gram_kernel(mine_ref, theirs_ref, out_ref, acc_ref)
    own_ref[...] = mine_ref[...]
    other_ref[...] = theirs_ref[...]


def pair_terms_stored(mine, theirs, own_full, other_full, chunk):
    width, piece = mine.shape
    cell_spec = pl.BlockSpec((width, piece), lambda step: (0, 0))
    full_spec = pl.BlockSpec((width, piece), lambda step: (0, chunk))
    return pl.pallas_call(
        gram_store_kernel,
        out_shape=[
            jax.ShapeDtypeStruct((2 * width + 8, width), jnp.float32),
            jax.ShapeDtypeStruct(own_full.shape, own_full.dtype),
            jax.ShapeDtypeStruct(other_full.shape, other_full.dtype),
        ],
        grid=(1,),
        in_specs=[cell_spec, cell_spec, pl.BlockSpec(memory_space=pl.ANY), pl.BlockSpec(memory_space=pl.ANY)],
        out_specs=[pl.BlockSpec((2 * width + 8, width), lambda step: (0, 0)), full_spec, full_spec],
        scratch_shapes=[pltpu.VMEM((2 * width, 2 * width), jnp.float32)],
        input_output_aliases={2: 1, 3: 2},
        cost_estimate=pl.CostEstimate(
            flops=8 * width * width * piece, transcendentals=0, bytes_accessed=16 * width * piece
        ),
    )(mine, theirs, own_full, other_full)


def mine_kernel(mine_ref, out_ref, acc_ref):
    step = pl.program_id(0)

    @pl.when(step == 0)
    def _():
        acc_ref[...] = jnp.zeros_like(acc_ref)

    acc_ref[...] += lax.dot_general(
        mine_ref[...],
        mine_ref[...],
        (((1,), (1,)), ((), ())),
        precision=lax.Precision.HIGHEST,
        preferred_element_type=jnp.float32,
    )

    @pl.when(step == pl.num_programs(0) - 1)
    def _():
        width = mine_ref.shape[0]
        row = lax.broadcasted_iota(jnp.int32, (width, width), 0)
        col = lax.broadcasted_iota(jnp.int32, (width, width), 1)
        out_ref[:width, :] = jnp.where(row <= col, acc_ref[...], 0.0)
        out_ref[width:, :] = jnp.zeros((width + 8, width), jnp.float32)


def rest_kernel(mine_ref, theirs_ref, out_ref, acc_ref):
    step = pl.program_id(0)

    @pl.when(step == 0)
    def _():
        acc_ref[...] = jnp.zeros_like(acc_ref)

    stacked = jnp.concatenate([mine_ref[...], theirs_ref[...]], 0)
    acc_ref[...] += lax.dot_general(
        stacked,
        theirs_ref[...],
        (((1,), (1,)), ((), ())),
        precision=lax.Precision.HIGHEST,
        preferred_element_type=jnp.float32,
    )

    @pl.when(step == pl.num_programs(0) - 1)
    def _():
        width = mine_ref.shape[0]
        row = lax.broadcasted_iota(jnp.int32, (width, width), 0)
        col = lax.broadcasted_iota(jnp.int32, (width, width), 1)
        gram_theirs = acc_ref[width:, :]
        out_ref[:width, :] = jnp.where(row > col, gram_theirs, 0.0)
        out_ref[width : 2 * width, :] = acc_ref[:width, :]
        diag_theirs = jnp.sum(jnp.where(row == col, gram_theirs, 0.0), axis=0, keepdims=True)
        out_ref[2 * width :, :] = jnp.broadcast_to(diag_theirs, (8, width))


def split_terms(kernel, operands, acc_rows):
    width, cells = operands[0].shape
    tile = min(cells, 2048)
    cell_spec = pl.BlockSpec((width, tile), lambda step: (0, step))
    return pl.pallas_call(
        kernel,
        out_shape=jax.ShapeDtypeStruct((2 * width + 8, width), jnp.float32),
        grid=(cells // tile,),
        in_specs=[cell_spec] * len(operands),
        out_specs=pl.BlockSpec((2 * width + 8, width), lambda step: (0, 0)),
        scratch_shapes=[pltpu.VMEM((acc_rows, width), jnp.float32)],
        cost_estimate=pl.CostEstimate(
            flops=2 * acc_rows * width * cells,
            transcendentals=0,
            bytes_accessed=4 * width * cells * len(operands),
        ),
    )(*operands)


def pair_terms(mine, theirs):
    width, cells = mine.shape
    tile = min(cells, 2048)
    cell_spec = pl.BlockSpec((width, tile), lambda step: (0, step))
    return pl.pallas_call(
        gram_kernel,
        out_shape=jax.ShapeDtypeStruct((2 * width + 8, width), jnp.float32),
        grid=(cells // tile,),
        in_specs=[cell_spec, cell_spec],
        out_specs=pl.BlockSpec((2 * width + 8, width), lambda step: (0, 0)),
        scratch_shapes=[pltpu.VMEM((2 * width, 2 * width), jnp.float32)],
        cost_estimate=pl.CostEstimate(
            flops=8 * width * width * cells, transcendentals=0, bytes_accessed=8 * width * cells
        ),
    )(mine, theirs)


def row_total(part):
    count = lax.axis_size("rows")
    bit = 1
    while bit < count:
        pairs = [(source, source ^ bit) for source in range(count)]
        part = part + lax.ppermute(part, "rows", pairs)
        bit *= 2
    return part


CHUNKS = 4


def lay_kernel(chunk_ids, piece, source_ref, *out_refs):
    if len(chunk_ids) == 1:
        out_refs[0][...] = source_ref[...]
        return
    for chunk, out_ref in zip(chunk_ids, out_refs):
        out_ref[...] = source_ref[:, chunk * piece : (chunk + 1) * piece]


def lay_out(snapshots, rows_n, chunks, chunk_ids):
    local_rows, cells = snapshots.shape
    width = cells // rows_n
    piece = width // chunks
    out_spec = pl.BlockSpec((None, local_rows, piece), lambda dest: (dest, 0, 0))
    return pl.pallas_call(
        functools.partial(lay_kernel, tuple(chunk_ids), piece),
        out_shape=[jax.ShapeDtypeStruct((rows_n, local_rows, piece), snapshots.dtype)] * len(chunk_ids),
        grid=(rows_n,),
        in_specs=[
            pl.BlockSpec((local_rows, piece), lambda dest: (0, dest * chunks + chunk_ids[0]))
            if len(chunk_ids) == 1
            else pl.BlockSpec((local_rows, width), lambda dest: (0, dest))
        ],
        out_specs=[out_spec] * len(chunk_ids),
        cost_estimate=pl.CostEstimate(
            flops=0, transcendentals=0, bytes_accessed=8 * local_rows * piece * rows_n * len(chunk_ids)
        ),
    )(snapshots)


def exchange(bit_pos, snapshots):
    chunks = 1 if bit_pos == 0 else CHUNKS
    rows_n = lax.axis_size("rows")
    local_rows, cells = snapshots.shape
    width = cells // rows_n
    piece = width // chunks

    if chunks == 1:
        mine = lax.all_to_all(snapshots, "rows", split_axis=1, concat_axis=0, tiled=True)
        block_rows = mine.shape[0]
        own_terms = split_terms(mine_kernel, (mine,), block_rows)
        theirs = partner_2(mine, "cols", bit_pos)
        return mine, theirs, own_terms + split_terms(rest_kernel, (mine, theirs), 2 * block_rows)

    sends = lay_out(snapshots, rows_n, chunks, [0]) + lay_out(snapshots, rows_n, chunks, list(range(1, chunks)))

    def laid(chunk):
        return sends[chunk]

    def spread(sent):
        got = lax.all_to_all(sent, "rows", split_axis=0, concat_axis=0)
        return got.reshape(rows_n * local_rows, piece)

    own_parts = [spread(laid(0))]
    other_parts = []
    for chunk in range(1, chunks):
        held = (own_parts[-1], laid(chunk)) + tuple(other_parts[-1:])
        held = lax.optimization_barrier(held)
        own_parts[-1] = held[0]
        if other_parts:
            other_parts[-1] = held[2]
        other_parts.append(partner_2(held[0], "cols", bit_pos))
        own_parts.append(spread(held[1]))
    other_parts.append(partner_2(own_parts[-1], "cols", bit_pos))
    own_full = jnp.zeros((rows_n * local_rows, width), snapshots.dtype)
    other_full = jnp.zeros((rows_n * local_rows, width), snapshots.dtype)
    terms = None
    for chunk, (mine, theirs) in enumerate(zip(own_parts, other_parts)):
        part, own_full, other_full = pair_terms_stored(mine, theirs, own_full, other_full, chunk)
        terms = part if terms is None else terms + part
    return own_full, other_full, terms


def unpack_terms(packed, width):
    row = lax.broadcasted_iota(jnp.int32, (width, width), 0)
    col = lax.broadcasted_iota(jnp.int32, (width, width), 1)
    shared = packed[:width]
    gram_mixed = packed[width : 2 * width]
    diag_theirs = packed[2 * width : 2 * width + 1]
    gram_mine = jnp.where(row <= col, shared, shared.T)
    gram_theirs = jnp.where(row > col, shared, jnp.where(row < col, shared.T, diag_theirs))
    return gram_mine, gram_mixed, gram_theirs


def assemble(terms, own_low):
    gram_mine, gram_mixed, gram_theirs = unpack_terms(row_total(terms), terms.shape[1])
    upper_left = jnp.where(own_low, gram_mine, gram_theirs)
    lower_right = jnp.where(own_low, gram_theirs, gram_mine)
    upper_right = jnp.where(own_low, gram_mixed, gram_mixed.T)
    top_rows = jnp.concatenate([upper_left, upper_right], 1)
    bottom_rows = jnp.concatenate([upper_right.T, lower_right], 1)
    return jnp.concatenate([top_rows, bottom_rows], 0)


def rotate_kernel(coef_ref, mine_ref, theirs_ref, out_ref):
    stacked = jnp.concatenate([mine_ref[...], theirs_ref[...]], 0)
    out_ref[...] = jnp.dot(
        coef_ref[...], stacked, precision=lax.Precision.HIGHEST, preferred_element_type=jnp.float32
    )


def rotate_part(columns_sel, own_low, mine, theirs):
    width, cells = mine.shape
    coef_mine = jnp.where(own_low, columns_sel[:width], columns_sel[width:])
    coef_theirs = jnp.where(own_low, columns_sel[width:], columns_sel[:width])
    coef = jnp.concatenate([coef_mine, coef_theirs], 0).T
    tile = min(cells, 2048)
    coef_spec = pl.BlockSpec((width, 2 * width), lambda step: (0, 0))
    cell_spec = pl.BlockSpec((width, tile), lambda step: (0, step))
    return pl.pallas_call(
        rotate_kernel,
        out_shape=jax.ShapeDtypeStruct((width, cells), jnp.float32),
        grid=(cells // tile,),
        in_specs=[coef_spec, cell_spec, cell_spec],
        out_specs=cell_spec,
        cost_estimate=pl.CostEstimate(
            flops=4 * width * width * cells, transcendentals=0, bytes_accessed=12 * width * cells
        ),
    )(coef, mine, theirs)


def shards(snapshots, pair_table):
    bit_count = lax.axis_size("cols").bit_length() - 1
    column = lax.axis_index("cols")
    mask_val = pair_table[0]
    bit_index = jnp.int32(0)
    for bit_pos in range(bit_count):
        bit_index = bit_index + (mask_val >> bit_pos & 1) * bit_pos
    partner = jnp.bitwise_xor(column, mask_val)
    own_low = column < partner
    branches = [functools.partial(exchange, bit_pos) for bit_pos in range(bit_count)]
    own_parts, other_parts, terms = lax.switch(bit_index, branches, snapshots)
    gram_full = assemble(terms, own_low)
    rotation = jacobi_pallas(gram_full)
    width = own_parts.shape[0]
    own_columns = jnp.where(own_low, rotation[:, :width], rotation[:, width:])
    return rotate_part(own_columns, own_low, own_parts, other_parts)


def solution(mesh):
    in_specs = (P(("cols", "rows"), None), P())
    out_specs = P("cols", "rows")
    return jax.shard_map(shards, mesh=mesh, in_specs=in_specs, out_specs=out_specs, check_vma=False)
```

profile of v0, /device:TPU:0, one launch (start us, length us, event | category | flops | bytes accessed | tf_op | source)
XLA Modules:
  0.0 161.7 jit_solution(841752920216883059)
XLA Ops:
  0.7 119.5 %conditional.1 = (f32[128,8192]{1,0:T(8,128)}, f32[128,8192]{1,0:T(8,128)}, f32[264,128]{1,0:T(8,128)S(1)}, f32[264,128]{1,0:T(8,128)S(1)}) conditional(s32[]{:T(128)} %clamp.3, f32[16,65536]{1,0:T(8,128)} %param.4, f32[16,65536]{1,0:T(8,128)} %param.4), branch_computations={%region_0.0_spmd, %region_1.0_spmd} | conditional | flops 1073809408 | bytes 77119960 | solution.py:367
  0.7 2.5 %copy.26 = f32[2,8,8,8192]{3,2,0,1:T(8,128)S(1)} copy(f32[2,8,8,8192]{3,2,1,0:T(8,128)} %bitcast.27) | data formatting | bytes 8388608 | tf_op jit(solution)/shard_map/cond/branch_0_fun/all_to_all | solution.py:274
  3.2 100.4 %all_to_all.31 = f32[16,8,8192]{2,0,1:T(8,128)} all-to-all(f32[16,8,8192]{2,0,1:T(8,128)S(1)} %bitcast.28), channel_id=1, replica_groups=mesh['rows'=8,'cols'=4] {'rows'}, dimensions={1} | all-to-all | bytes 8388608 | tf_op jit(solution)/shard_map/cond/branch_0_fun/all_to_all | solution.py:274
  103.5 5.5 %branch_0_fun.2 = f32[264,128]{1,0:T(8,128)S(1)} custom-call(f32[128,8192]{1,0:T(8,128)} %bitcast.1.mine_ref), custom_call_target="tpu_custom_call" | custom-call | flops 268435456 | bytes 4194304 | tf_op jit(solution)/shard_map/cond/branch_0_fun/pallas_call | solution.py:192
  109.1 1.9 %collective-permute-done.theirs_ref = f32[128,8192]{1,0:T(8,128)} collective-permute-done((f32[128,8192]{1,0:T(8,128)}, f32[128,8192]{1,0:T(8,128)}, u32[]{:S(2)}, u32[]{:S(2)}) %collective-permute-start) | collective-permute-done | bytes 4194336 | tf_op jit(solution)/shard_map/cond/branch_0_fun/ppermute | solution.py:17
  111.0 8.9 %branch_0_fun.3 = f32[264,128]{1,0:T(8,128)S(1)} custom-call(f32[128,8192]{1,0:T(8,128)} %bitcast.1.mine_ref, f32[128,8192]{1,0:T(8,128)} %collective-permute-done.theirs_ref), custom_call_target="tpu_custom_call" | custom-call | flops 536870912 | bytes 8388608 | tf_op jit(solution)/shard_map/cond/branch_0_fun/pallas_call | solution.py:192
  120.2 1.5 collective-permute-start.5
  121.7 4.2 %collective-permute-done.5 = f32[264,128]{1,0:T(8,128)S(1)} collective-permute-done((f32[264,128]{1,0:T(8,128)S(1)}, f32[264,128]{1,0:T(8,128)S(1)}, u32[]{:S(2)}, u32[]{:S(2)}) %collective-permute-start.5) | collective-permute-done | bytes 135200 | tf_op jit(solution)/shard_map/ppermute | solution.py:229
  125.9 1.2 collective-permute-start.6
  127.1 3.9 %collective-permute-done.6 = f32[264,128]{1,0:T(8,128)S(1)} collective-permute-done((f32[264,128]{1,0:T(8,128)S(1)}, f32[264,128]{1,0:T(8,128)S(1)}, u32[]{:S(2)}, u32[]{:S(2)}) %collective-permute-start.6) | collective-permute-done | bytes 135200 | tf_op jit(solution)/shard_map/ppermute | solution.py:229
  131.0 1.1 collective-permute-start.7
  132.2 6.3 %collective-permute-done.7 = f32[264,128]{1,0:T(8,128)S(1)} collective-permute-done((f32[264,128]{1,0:T(8,128)S(1)}, f32[264,128]{1,0:T(8,128)S(1)}, u32[]{:S(2)}, u32[]{:S(2)}) %collective-permute-start.7) | collective-permute-done | bytes 135200 | tf_op jit(solution)/shard_map/ppermute | solution.py:229
  138.7 0.1 copy.14
  138.8 0.1 copy.16
  138.9 0.1 copy.17
  139.0 0.1 copy.18
  139.1 0.1 copy.15
  139.3 0.8 copy.19.gram_ref
  140.1 11.8 %shard_map.34 = f32[256,256]{1,0:T(8,128)} custom-call(f32[256,256]{1,0:T(8,128)} %copy.19.gram_ref), custom_call_target="tpu_custom_call" | custom-call | tf_op jit(solution)/shard_map/pallas_call | solution.py:71
  151.9 1.0 fusion.2
  152.9 0.1 copy.22
  153.0 0.1 copy.23
  153.1 0.7 maximum_bitcast_fusion.coef_ref
  153.8 7.9 %shard_map.35 = f32[128,8192]{1,0:T(8,128)} custom-call(f32[128,256]{1,0:T(8,128)} %maximum_bitcast_fusion.coef_ref, f32[128,8192]{1,0:T(8,128)} %get-tuple-element.40.mine_ref, f32[128,8192]{1,0:T(8,128)} %get-tuple-element.41.theirs_ref), custom_call_target="tpu_custom_call" | custom-call | flops 536870912 | bytes 12582912 | tf_op jit(solution)/shard_map/pallas_call | solution.py:345
  (15 shorter events, 0.3 us)
Async XLA Ops:
  0.7 131.5 %copy-start.5 = (s32[4]{0:T(128)S(1)}, s32[4]{0:T(128)}, u32[]{:S(2)}) copy-start(s32[4]{0:T(128)} %param.5) | copy-start | bytes 52
  103.5 7.5 %collective-permute-start = (f32[128,8192]{1,0:T(8,128)}, f32[128,8192]{1,0:T(8,128)}, u32[]{:S(2)}, u32[]{:S(2)}) collective-permute-start(f32[128,8192]{1,0:T(8,128)} %bitcast.1.mine_ref), channel_id=1, source_target_pairs={{0,1},{1,0},{2,3},{3,2},{4,5},{5,4},{6,7},{7,6},{8,9},{9,8},{10,11... | collective-permute-start | bytes 12582920 | tf_op jit(solution)/shard_map/cond/branch_0_fun/ppermute | solution.py:17
  120.2 5.7 %collective-permute-start.5 = (f32[264,128]{1,0:T(8,128)S(1)}, f32[264,128]{1,0:T(8,128)S(1)}, u32[]{:S(2)}, u32[]{:S(2)}) collective-permute-start(f32[264,128]{1,0:T(8,128)S(1)} %add.20), channel_id=1, source_target_pairs={{0,4},{4,0},{8,12},{12,8},{16,20},{20,16},{24,28},{28,24},{1,5},{5... | collective-permute-start | bytes 405512 | tf_op jit(solution)/shard_map/ppermute | solution.py:229
  125.9 5.1 %collective-permute-start.6 = (f32[264,128]{1,0:T(8,128)S(1)}, f32[264,128]{1,0:T(8,128)S(1)}, u32[]{:S(2)}, u32[]{:S(2)}) collective-permute-start(f32[264,128]{1,0:T(8,128)S(1)} %add.21), channel_id=1, source_target_pairs={{0,8},{4,12},{8,0},{12,4},{16,24},{20,28},{24,16},{28,20},{1,9},{5... | collective-permute-start | bytes 405512 | tf_op jit(solution)/shard_map/ppermute | solution.py:229
  131.0 7.5 %collective-permute-start.7 = (f32[264,128]{1,0:T(8,128)S(1)}, f32[264,128]{1,0:T(8,128)S(1)}, u32[]{:S(2)}, u32[]{:S(2)}) collective-permute-start(f32[264,128]{1,0:T(8,128)S(1)} %add.22), channel_id=1, source_target_pairs={{0,16},{4,20},{8,24},{12,28},{16,0},{20,4},{24,8},{28,12},{1,17},{... | collective-permute-start | bytes 405512 | tf_op jit(solution)/shard_map/ppermute | solution.py:229
where the time goes:
time: 162 us
  blocking collectives  100 us (62%)
  Pallas kernels  34.1 us (21%)
  waiting for transfers between devices  16.4 us (10%)
  local copies, waits for them, and re-layouts  5.06 us (3%)
  starting transfers between devices  3.82 us (2%)
    all_to_all x1, blocking collectives, exchange(): lax.all_to_all(snapshots, 'rows', split_axis=1, concat_axis=0, tiled=True)  100 us
    pallas_call x2, Pallas kernels, split_terms(): pl.pallas_call(kernel, out_shape=jax.ShapeDtypeStruct((2 * width + 8, wid...  14.5 us
    ppermute x3, waiting for transfers between devices, row_total(): part = part + lax.ppermute(part, 'rows', pairs)  14.4 us
    pallas_call x1, Pallas kernels, jacobi_pallas(): pl.pallas_call(jacobi_kernel, out_shape=jax.ShapeDtypeStruct(gram.shape,...  11.8 us
    pallas_call x1, Pallas kernels, rotate_part(): pl.pallas_call(rotate_kernel, out_shape=jax.ShapeDtypeStruct((width, cell...  7.9 us
    ppermute x3, starting transfers between devices, row_total(): part = part + lax.ppermute(part, 'rows', pairs)  3.82 us
  transfers between devices with their start and end apart: 4, of which 4 were waited for; matrix products, arithmetic and copies ran while one was open for 0% of the time, Pallas kernels for 3%

commit v1 on v0

--- a/solution.py
+++ b/solution.py
@@ -111,12 +111,21 @@
     other_ref[...] = theirs_ref[...]
 
 
-def pair_terms_stored(mine, theirs, own_full, other_full, chunk):
+def rest_store_kernel(mine_ref, theirs_ref, own_in, other_in, out_ref, own_ref, other_ref, acc_ref):
+    del own_in, other_in
+    rest_kernel(mine_ref, theirs_ref, out_ref, acc_ref)
+    own_ref[...] = mine_ref[...]
+    other_ref[...] = theirs_ref[...]
+
+
+def pair_terms_stored(mine, theirs, own_full, other_full, chunk, kernel=None, acc_rows=None):
     width, piece = mine.shape
+    kernel = gram_store_kernel if kernel is None else kernel
+    acc_shape = (2 * width, 2 * width) if acc_rows is None else (acc_rows, width)
     cell_spec = pl.BlockSpec((width, piece), lambda step: (0, 0))
     full_spec = pl.BlockSpec((width, piece), lambda step: (0, chunk))
     return pl.pallas_call(
-        gram_store_kernel,
+        kernel,
         out_shape=[
             jax.ShapeDtypeStruct((2 * width + 8, width), jnp.float32),
             jax.ShapeDtypeStruct(own_full.shape, own_full.dtype),
@@ -125,7 +134,7 @@
         grid=(1,),
         in_specs=[cell_spec, cell_spec, pl.BlockSpec(memory_space=pl.ANY), pl.BlockSpec(memory_space=pl.ANY)],
         out_specs=[pl.BlockSpec((2 * width + 8, width), lambda step: (0, 0)), full_spec, full_spec],
-        scratch_shapes=[pltpu.VMEM((2 * width, 2 * width), jnp.float32)],
+        scratch_shapes=[pltpu.VMEM(acc_shape, jnp.float32)],
         input_output_aliases={2: 1, 3: 2},
         cost_estimate=pl.CostEstimate(
             flops=8 * width * width * piece, transcendentals=0, bytes_accessed=16 * width * piece
@@ -296,13 +305,20 @@
             other_parts[-1] = held[2]
         other_parts.append(partner_2(held[0], "cols", bit_pos))
         own_parts.append(spread(held[1]))
+    block_rows = rows_n * local_rows
+    last_own = split_terms(mine_kernel, (own_parts[-1],), block_rows)
     other_parts.append(partner_2(own_parts[-1], "cols", bit_pos))
-    own_full = jnp.zeros((rows_n * local_rows, width), snapshots.dtype)
-    other_full = jnp.zeros((rows_n * local_rows, width), snapshots.dtype)
-    terms = None
+    own_full = jnp.zeros((block_rows, width), snapshots.dtype)
+    other_full = jnp.zeros((block_rows, width), snapshots.dtype)
+    terms = last_own
     for chunk, (mine, theirs) in enumerate(zip(own_parts, other_parts)):
-        part, own_full, other_full = pair_terms_stored(mine, theirs, own_full, other_full, chunk)
-        terms = part if terms is None else terms + part
+        if chunk == chunks - 1:
+            part, own_full, other_full = pair_terms_stored(
+                mine, theirs, own_full, other_full, chunk, rest_store_kernel, 2 * block_rows
+            )
+        else:
+            part, own_full, other_full = pair_terms_stored(mine, theirs, own_full, other_full, chunk)
+        terms = terms + part
     return own_full, other_full, terms
 
 

time: 162 us -> 199 us (1.23)
  blocking collectives: 100 us -> 0 us
  waiting for transfers between devices: 16.4 us -> 107 us
  starting transfers between devices: 3.82 us -> 27.4 us
  Pallas kernels: 34.1 us -> 53.2 us
  local copies, waits for them, and re-layouts: 5.06 us -> 8.44 us
    all_to_all x1 -> x0, blocking collectives: 100 us -> none  [exchange(): lax.all_to_all(snapshots, 'rows', split_axis=1, concat_axis=0, tiled=True)]
    all_to_all x0 -> x4, waiting for transfers between devices: none -> 45.3 us  [spread(): got = lax.all_to_all(sent, 'rows', split_axis=0, concat_axis=0)]
    ppermute x1 -> x4, waiting for transfers between devices: 1.95 us -> 45.7 us  [partner_2(): return lax.ppermute(value, axis, pairs)]
    pallas_call x0 -> x6, Pallas kernels: none -> 30.6 us  [the longest x4 19.1 us: pair_terms_stored(): pl.pallas_call(kernel, out_shape=[jax.ShapeDtypeStruct((2 * width + 8, wi...]
    all_to_all x0 -> x4, starting transfers between devices: none -> 20 us  [spread(): got = lax.all_to_all(sent, 'rows', split_axis=0, concat_axis=0)]
    pallas_call x2 -> x1, Pallas kernels: 14.5 us -> 2.91 us  [split_terms(): pl.pallas_call(kernel, out_shape=jax.ShapeDtypeStruct((2 * width + 8, wid...]
    ppermute x1 -> x4, starting transfers between devices: 0.01 us -> 6.01 us  [partner_2(): return lax.ppermute(value, axis, pairs)]
    another operation x0 -> x2, local copies, waits for them, and re-layouts: none -> 4.85 us
  transfers between devices with their start and end apart: 4 -> 11, of which waited for: 4 -> 9; matrix products, arithmetic and copies ran while one was open for 0% -> 3% of each run, Pallas kernels for 3% -> 12%
where the time goes in v1:
time: 199 us; the launch traced here: 198 us
  waiting for transfers between devices  107 us (54%)
  Pallas kernels  53.2 us (27%)
  starting transfers between devices  27.4 us (14%)
  local copies, waits for them, and re-layouts  8.44 us (4%)
    ppermute x4, waiting for transfers between devices, partner_2(): return lax.ppermute(value, axis, pairs)  45.7 us
    all_to_all x4, waiting for transfers between devices, spread(): got = lax.all_to_all(sent, 'rows', split_axis=0, concat_axis=0)  45.3 us
    all_to_all x4, starting transfers between devices, spread(): got = lax.all_to_all(sent, 'rows', split_axis=0, concat_axis=0)  20 us
    pallas_call x4, Pallas kernels, pair_terms_stored(): pl.pallas_call(kernel, out_shape=[jax.ShapeDtypeStruct((2 * width + 8, wi...  19.1 us
    ppermute x3, waiting for transfers between devices, row_total(): part = part + lax.ppermute(part, 'rows', pairs)  15.6 us
    pallas_call x1, Pallas kernels, jacobi_pallas(): pl.pallas_call(jacobi_kernel, out_shape=jax.ShapeDtypeStruct(gram.shape,...  11.8 us
    pallas_call x2, Pallas kernels, lay_out(): pl.pallas_call(functools.partial(lay_kernel, tuple(chunk_ids), piece), ou...  11.5 us
    pallas_call x1, Pallas kernels, rotate_part(): pl.pallas_call(rotate_kernel, out_shape=jax.ShapeDtypeStruct((width, cell...  7.9 us
  transfers between devices with their start and end apart: 11, of which 9 were waited for; matrix products, arithmetic and copies ran while one was open for 3% of the time, Pallas kernels for 12%

profile of v1, /device:TPU:0, one launch (start us, length us, event | category | flops | bytes accessed | tf_op | source)
XLA Modules:
  0.0 198.5 jit_solution(1715150192423644385)
XLA Ops:
  0.7 157.5 %conditional.1 = (f32[128,8192]{1,0:T(8,128)}, f32[128,8192]{1,0:T(8,128)}, f32[264,128]{1,0:T(8,128)S(1)}, f32[264,128]{1,0:T(8,128)S(1)}) conditional(s32[]{:T(128)} %clamp.3, f32[16,65536]{1,0:T(8,128)} %param.4, f32[16,65536]{1,0:T(8,128)} %param.4), branch_computations={%region_0.0_spmd, %region_1.0_spmd} | conditional | flops 1140952064 | bytes 82498040 | solution.py:383
  0.7 5.2 %branch_1_fun.7 = f32[8,16,2048]{2,1,0:T(8,128)} custom-call(f32[16,65536]{1,0:T(8,128)} %source_ref.1), custom_call_target="tpu_custom_call" | custom-call | bytes 2097152 | tf_op jit(solution)/shard_map/cond/branch_1_fun/pallas_call | solution.py:259
  5.9 7.3 %all-to-all-start.1 = ((f32[8,16,2048]{2,1,0:T(8,128)}), f32[8,16,2048]{2,1,0:T(8,128)S(1)}, u32[]{:S(2)}, u32[]{:S(2)}) async-start(f32[8,16,2048]{2,1,0:T(8,128)} %branch_1_fun.7), calls=%async_computation.1 | async-start | bytes 2097152 | tf_op jit(solution)/shard_map/cond/branch_1_fun/all_to_all | solution.py:295
  13.1 6.3 %branch_1_fun.8 = (f32[8,16,2048]{2,1,0:T(8,128)}, f32[8,16,2048]{2,1,0:T(8,128)}, f32[8,16,2048]{2,1,0:T(8,128)}) custom-call(f32[16,65536]{1,0:T(8,128)} %source_ref.1), custom_call_target="tpu_custom_call" | custom-call | bytes 6291456 | tf_op jit(solution)/shard_map/cond/branch_1_fun/pallas_call | solution.py:259
  19.5 19.4 %all-to-all-done.1 = f32[8,16,2048]{2,1,0:T(8,128)S(1)} async-done(((f32[8,16,2048]{2,1,0:T(8,128)}), f32[8,16,2048]{2,1,0:T(8,128)S(1)}, u32[]{:S(2)}, u32[]{:S(2)}) %all-to-all-start.1) | async-done | bytes 1048608 | tf_op jit(solution)/shard_map/cond/branch_1_fun/all_to_all | solution.py:295
  38.9 3.6 %all-to-all-start.2 = ((f32[8,16,2048]{2,1,0:T(8,128)}), f32[8,16,2048]{2,1,0:T(8,128)S(1)}, u32[]{:S(2)}, u32[]{:S(2)}) async-start(f32[8,16,2048]{2,1,0:T(8,128)} %get-tuple-element.12), calls=%async_computation.2 | async-start | bytes 2097152 | tf_op jit(solution)/shard_map/cond/branch_1_fun/all_to_all | solution.py:295
  42.5 1.5 collective-permute-start.1
  44.0 23.4 %collective-permute-done.1.theirs_ref = f32[128,2048]{1,0:T(8,128)} collective-permute-done((f32[128,2048]{1,0:T(8,128)S(1)}, f32[128,2048]{1,0:T(8,128)}, u32[]{:S(2)}, u32[]{:S(2)}) %collective-permute-start.1) | collective-permute-done | bytes 1048608 | tf_op jit(solution)/shard_map/cond/branch_1_fun/ppermute | solution.py:17
  68.5 4.7 %all-to-all-start.3 = ((f32[8,16,2048]{2,1,0:T(8,128)}), f32[8,16,2048]{2,1,0:T(8,128)S(1)}, u32[]{:S(2)}, u32[]{:S(2)}) async-start(f32[8,16,2048]{2,1,0:T(8,128)} %get-tuple-element.15), calls=%async_computation.3 | async-start | bytes 2097152 | tf_op jit(solution)/shard_map/cond/branch_1_fun/all_to_all | solution.py:295
  74.6 22.4 %collective-permute-done.2.theirs_ref = f32[128,2048]{1,0:T(8,128)} collective-permute-done((f32[128,2048]{1,0:T(8,128)S(1)}, f32[128,2048]{1,0:T(8,128)}, u32[]{:S(2)}, u32[]{:S(2)}) %collective-permute-start.2) | collective-permute-done | bytes 1048608 | tf_op jit(solution)/shard_map/cond/branch_1_fun/ppermute | solution.py:17
  99.3 4.5 %all-to-all-start.4 = ((f32[8,16,2048]{2,1,0:T(8,128)}), f32[8,16,2048]{2,1,0:T(8,128)S(1)}, u32[]{:S(2)}, u32[]{:S(2)}) async-start(f32[8,16,2048]{2,1,0:T(8,128)} %get-tuple-element.18), calls=%async_computation.4 | async-start | bytes 2097152 | tf_op jit(solution)/shard_map/cond/branch_1_fun/all_to_all | solution.py:295
  105.2 23.6 %all-to-all-done.4 = f32[8,16,2048]{2,1,0:T(8,128)S(1)} async-done(((f32[8,16,2048]{2,1,0:T(8,128)}), f32[8,16,2048]{2,1,0:T(8,128)S(1)}, u32[]{:S(2)}, u32[]{:S(2)}) %all-to-all-start.4) | async-done | bytes 1048608 | tf_op jit(solution)/shard_map/cond/branch_1_fun/all_to_all | solution.py:295
  130.3 2.4 %broadcast_1_own_in_other_in.0.own_in = f32[128,8192]{1,0:T(8,128)} broadcast(f32[]{:T(128)} %constant.4.clone), dimensions={} | broadcast | bytes 4194308 | tf_op jit(solution)/shard_map/broadcast.1.own_in.other_in
  132.7 2.5 %broadcast_1_own_in_other_in.0.clone.other_in = f32[128,8192]{1,0:T(8,128)} broadcast(f32[]{:T(128)} %constant.4.clone), dimensions={} | broadcast | bytes 4194308 | tf_op jit(solution)/shard_map/broadcast.1.own_in.other_in
  135.2 4.8 %branch_1_fun.9 = (f32[264,128]{1,0:T(8,128)}, f32[128,8192]{1,0:T(8,128)}, f32[128,8192]{1,0:T(8,128)}) custom-call(f32[128,2048]{1,0:T(8,128)} %bitcast.33, f32[128,2048]{1,0:T(8,128)} %collective-permute-done.1.theirs_ref, f32[128,8192]{1,0:T(8,128)} %broadcast_1_own_in_other_in.0.own_in, ...), custom_call_target="tpu_custom_call", output_to_operand_aliasing={{1}: (2, {}), {2}: (3, {})} | custom-call | flops 268435456 | bytes 4194304 | tf_op jit(solution)/shard_map/cond/branch_1_fun/pallas_call | solution.py:127
  139.9 4.8 %branch_1_fun.10 = (f32[264,128]{1,0:T(8,128)}, f32[128,8192]{1,0:T(8,128)}, f32[128,8192]{1,0:T(8,128)}) custom-call(f32[128,2048]{1,0:T(8,128)} %bitcast.35, f32[128,2048]{1,0:T(8,128)} %collective-permute-done.2.theirs_ref, f32[128,8192]{1,0:T(8,128)} %get-tuple-element.22.own_in, ...), custom_call_target="tpu_custom_call", output_to_operand_aliasing={{1}: (2, {}), {2}: (3, {})} | custom-call | flops 268435456 | bytes 4194304 | tf_op jit(solution)/shard_map/cond/branch_1_fun/pallas_call | solution.py:127
  144.7 4.8 %branch_1_fun.11 = (f32[264,128]{1,0:T(8,128)}, f32[128,8192]{1,0:T(8,128)}, f32[128,8192]{1,0:T(8,128)}) custom-call(f32[128,2048]{1,0:T(8,128)} %bitcast.37, f32[128,2048]{1,0:T(8,128)} %collective-permute-done.4.theirs_ref, f32[128,8192]{1,0:T(8,128)} %get-tuple-element.24.own_in, ...), custom_call_target="tpu_custom_call", output_to_operand_aliasing={{1}: (2, {}), {2}: (3, {})} | custom-call | flops 268435456 | bytes 4194304 | tf_op jit(solution)/shard_map/cond/branch_1_fun/pallas_call | solution.py:127
  149.5 2.9 %branch_1_fun.13 = f32[264,128]{1,0:T(8,128)} custom-call(f32[128,2048]{1,0:T(8,128)} %bitcast.30), custom_call_target="tpu_custom_call" | custom-call | flops 67108864 | bytes 1048576 | tf_op jit(solution)/shard_map/cond/branch_1_fun/pallas_call | solution.py:201
  153.4 4.7 %branch_1_fun.12 = (f32[264,128]{1,0:T(8,128)S(1)}, f32[128,8192]{1,0:T(8,128)}, f32[128,8192]{1,0:T(8,128)}) custom-call(f32[128,2048]{1,0:T(8,128)} %bitcast.31, f32[128,2048]{1,0:T(8,128)} %collective-permute-done.3.theirs_ref, f32[128,8192]{1,0:T(8,128)} %get-tuple-element.26.own_in, ...), custom_call_target="tpu_custom_call", output_to_operand_aliasing={{1}: (2, {}), {2}: (3, {})} | custom-call | flops 268435456 | bytes 4194304 | tf_op jit(solution)/shard_map/cond/branch_1_fun/pallas_call | solution.py:127
  159.5 3.8 %collective-permute-done.5 = f32[264,128]{1,0:T(8,128)S(1)} collective-permute-done((f32[264,128]{1,0:T(8,128)S(1)}, f32[264,128]{1,0:T(8,128)S(1)}, u32[]{:S(2)}, u32[]{:S(2)}) %collective-permute-start.5) | collective-permute-done | bytes 135200 | tf_op jit(solution)/shard_map/ppermute | solution.py:238
  163.4 5.0 %collective-permute-done.6 = f32[264,128]{1,0:T(8,128)S(1)} collective-permute-done((f32[264,128]{1,0:T(8,128)S(1)}, f32[264,128]{1,0:T(8,128)S(1)}, u32[]{:S(2)}, u32[]{:S(2)}) %collective-permute-start.6) | collective-permute-done | bytes 135200 | tf_op jit(solution)/shard_map/ppermute | solution.py:238
  168.6 6.8 %collective-permute-done.7 = f32[264,128]{1,0:T(8,128)S(1)} collective-permute-done((f32[264,128]{1,0:T(8,128)S(1)}, f32[264,128]{1,0:T(8,128)S(1)}, u32[]{:S(2)}, u32[]{:S(2)}) %collective-permute-start.7) | collective-permute-done | bytes 135200 | tf_op jit(solution)/shard_map/ppermute | solution.py:238
  176.9 11.8 %shard_map.34 = f32[256,256]{1,0:T(8,128)} custom-call(f32[256,256]{1,0:T(8,128)} %copy.19.gram_ref), custom_call_target="tpu_custom_call" | custom-call | tf_op jit(solution)/shard_map/pallas_call | solution.py:71
  190.6 7.9 %shard_map.35 = f32[128,8192]{1,0:T(8,128)} custom-call(f32[128,256]{1,0:T(8,128)} %maximum_bitcast_fusion.coef_ref, f32[128,8192]{1,0:T(8,128)} %get-tuple-element.40.mine_ref, f32[128,8192]{1,0:T(8,128)} %get-tuple-element.41.theirs_ref), custom_call_target="tpu_custom_call" | custom-call | flops 536870912 | bytes 12582912 | tf_op jit(solution)/shard_map/pallas_call | solution.py:361
  (47 shorter events, 13.6 us)
Async XLA Ops:
  0.7 167.9 %copy-start.6 = (s32[4]{0:T(128)S(1)}, s32[4]{0:T(128)}, u32[]{:S(2)}) copy-start(s32[4]{0:T(128)} %param.5) | copy-start | bytes 52
  5.9 33.0 %all-to-all-start.1 = ((f32[8,16,2048]{2,1,0:T(8,128)}), f32[8,16,2048]{2,1,0:T(8,128)S(1)}, u32[]{:S(2)}, u32[]{:S(2)}) async-start(f32[8,16,2048]{2,1,0:T(8,128)} %branch_1_fun.7), calls=%async_computation.1 | async-start | bytes 2097152 | tf_op jit(solution)/shard_map/cond/branch_1_fun/all_to_all | solution.py:295
  38.9 93.8 %copy-start.1 = (f32[8,16,2048]{2,1,0:T(8,128)}, f32[8,16,2048]{2,1,0:T(8,128)S(1)}, u32[]{:S(2)}) copy-start(f32[8,16,2048]{2,1,0:T(8,128)S(1)} %all-to-all-done.1) | copy-start | bytes 3145732 | tf_op jit(solution)/shard_map/cond
  38.9 29.5 %all-to-all-start.2 = ((f32[8,16,2048]{2,1,0:T(8,128)}), f32[8,16,2048]{2,1,0:T(8,128)S(1)}, u32[]{:S(2)}, u32[]{:S(2)}) async-start(f32[8,16,2048]{2,1,0:T(8,128)} %get-tuple-element.12), calls=%async_computation.2 | async-start | bytes 2097152 | tf_op jit(solution)/shard_map/cond/branch_1_fun/all_to_all | solution.py:295
  42.5 24.9 %collective-permute-start.1 = (f32[128,2048]{1,0:T(8,128)S(1)}, f32[128,2048]{1,0:T(8,128)}, u32[]{:S(2)}, u32[]{:S(2)}) collective-permute-start(f32[128,2048]{1,0:T(8,128)S(1)} %bitcast.32), channel_id=1, source_target_pairs={{0,2},{1,3},{2,0},{3,1},{4,6},{5,7},{6,4},{7,5},{8,10},{9,11},{10,... | collective-permute-start | bytes 3145736 | tf_op jit(solution)/shard_map/cond/branch_1_fun/ppermute | solution.py:17
  68.5 64.2 %copy-start.2 = (f32[8,16,2048]{2,1,0:T(8,128)}, f32[8,16,2048]{2,1,0:T(8,128)S(1)}, u32[]{:S(2)}) copy-start(f32[8,16,2048]{2,1,0:T(8,128)S(1)} %all-to-all-done.2) | copy-start | bytes 3145732 | tf_op jit(solution)/shard_map/cond
  68.5 29.8 %all-to-all-start.3 = ((f32[8,16,2048]{2,1,0:T(8,128)}), f32[8,16,2048]{2,1,0:T(8,128)S(1)}, u32[]{:S(2)}, u32[]{:S(2)}) async-start(f32[8,16,2048]{2,1,0:T(8,128)} %get-tuple-element.15), calls=%async_computation.3 | async-start | bytes 2097152 | tf_op jit(solution)/shard_map/cond/branch_1_fun/all_to_all | solution.py:295
  73.1 23.9 %collective-permute-start.2 = (f32[128,2048]{1,0:T(8,128)S(1)}, f32[128,2048]{1,0:T(8,128)}, u32[]{:S(2)}, u32[]{:S(2)}) collective-permute-start(f32[128,2048]{1,0:T(8,128)S(1)} %bitcast.34), channel_id=1, source_target_pairs={{0,2},{1,3},{2,0},{3,1},{4,6},{5,7},{6,4},{7,5},{8,10},{9,11},{10,... | collective-permute-start | bytes 3145736 | tf_op jit(solution)/shard_map/cond/branch_1_fun/ppermute | solution.py:17
  98.3 1.0 copy-start.3
  99.3 29.5 %all-to-all-start.4 = ((f32[8,16,2048]{2,1,0:T(8,128)}), f32[8,16,2048]{2,1,0:T(8,128)S(1)}, u32[]{:S(2)}, u32[]{:S(2)}) async-start(f32[8,16,2048]{2,1,0:T(8,128)} %get-tuple-element.18), calls=%async_computation.4 | async-start | bytes 2097152 | tf_op jit(solution)/shard_map/cond/branch_1_fun/all_to_all | solution.py:295
  103.7 41.0 %collective-permute-start.4 = (f32[128,2048]{1,0:T(8,128)}, f32[128,2048]{1,0:T(8,128)}, u32[]{:S(2)}, u32[]{:S(2)}) collective-permute-start(f32[128,2048]{1,0:T(8,128)} %bitcast.36), channel_id=1, source_target_pairs={{0,2},{1,3},{2,0},{3,1},{4,6},{5,7},{6,4},{7,5},{8,10},{9,11},{10,... | collective-permute-start | bytes 3145736 | tf_op jit(solution)/shard_map/cond/branch_1_fun/ppermute | solution.py:17
  128.8 6.4 %copy-start = (f32[8,16,2048]{2,1,0:T(8,128)}, f32[8,16,2048]{2,1,0:T(8,128)S(1)}, u32[]{:S(2)}) copy-start(f32[8,16,2048]{2,1,0:T(8,128)S(1)} %all-to-all-done.4) | copy-start | bytes 3145732 | tf_op jit(solution)/shard_map/cond
  128.8 24.6 %collective-permute-start.3 = (f32[128,2048]{1,0:T(8,128)S(1)}, f32[128,2048]{1,0:T(8,128)}, u32[]{:S(2)}, u32[]{:S(2)}) collective-permute-start(f32[128,2048]{1,0:T(8,128)S(1)} %bitcast.29), channel_id=1, source_target_pairs={{0,2},{1,3},{2,0},{3,1},{4,6},{5,7},{6,4},{7,5},{8,10},{9,11},{10,... | collective-permute-start | bytes 3145736 | tf_op jit(solution)/shard_map/cond/branch_1_fun/ppermute | solution.py:17
  144.7 7.7 %copy-start.4 = (f32[264,128]{1,0:T(8,128)S(1)}, f32[264,128]{1,0:T(8,128)}, u32[]{:S(2)}) copy-start(f32[264,128]{1,0:T(8,128)} %get-tuple-element.30) | copy-start | bytes 405508 | tf_op jit(solution)/shard_map/cond
  144.7 7.7 %copy-start.5 = (f32[264,128]{1,0:T(8,128)S(1)}, f32[264,128]{1,0:T(8,128)}, u32[]{:S(2)}) copy-start(f32[264,128]{1,0:T(8,128)} %get-tuple-element.31) | copy-start | bytes 405508 | tf_op jit(solution)/shard_map/cond
  158.2 5.1 %collective-permute-start.5 = (f32[264,128]{1,0:T(8,128)S(1)}, f32[264,128]{1,0:T(8,128)S(1)}, u32[]{:S(2)}, u32[]{:S(2)}) collective-permute-start(f32[264,128]{1,0:T(8,128)S(1)} %add.23), channel_id=1, source_target_pairs={{0,4},{4,0},{8,12},{12,8},{16,20},{20,16},{24,28},{28,24},{1,5},{5... | collective-permute-start | bytes 405512 | tf_op jit(solution)/shard_map/ppermute | solution.py:238
  163.3 5.1 %collective-permute-start.6 = (f32[264,128]{1,0:T(8,128)S(1)}, f32[264,128]{1,0:T(8,128)S(1)}, u32[]{:S(2)}, u32[]{:S(2)}) collective-permute-start(f32[264,128]{1,0:T(8,128)S(1)} %add.24), channel_id=1, source_target_pairs={{0,8},{4,12},{8,0},{12,4},{16,24},{20,28},{24,16},{28,20},{1,9},{5... | collective-permute-start | bytes 405512 | tf_op jit(solution)/shard_map/ppermute | solution.py:238
  168.4 6.9 %collective-permute-start.7 = (f32[264,128]{1,0:T(8,128)S(1)}, f32[264,128]{1,0:T(8,128)S(1)}, u32[]{:S(2)}, u32[]{:S(2)}) collective-permute-start(f32[264,128]{1,0:T(8,128)S(1)} %add.25), channel_id=1, source_target_pairs={{0,16},{4,20},{8,24},{12,28},{16,0},{20,4},{24,8},{28,12},{1,17},{... | collective-permute-start | bytes 405512 | tf_op jit(solution)/shard_map/ppermute | solution.py:238

commit v2 on v0

--- a/solution.py
+++ b/solution.py
@@ -17,12 +17,30 @@
     return lax.ppermute(value, axis, pairs)
 
 
-def jacobi_kernel(gram_ref, rotation_ref):
+def packed_gram(low, packed):
+    width = packed.shape[1]
+    row = lax.broadcasted_iota(jnp.int32, (width, width), 0)
+    col = lax.broadcasted_iota(jnp.int32, (width, width), 1)
+    shared = packed[:width]
+    shared_t = shared.T
+    gram_mixed = packed[width : 2 * width]
+    diag_theirs = packed[2 * width : 2 * width + 1]
+    gram_mine = jnp.where(row <= col, shared, shared_t)
+    gram_theirs = jnp.where(row > col, shared, jnp.where(row < col, shared_t, diag_theirs))
+    upper_left = jnp.where(low, gram_mine, gram_theirs)
+    lower_right = jnp.where(low, gram_theirs, gram_mine)
+    upper_right = jnp.where(low, gram_mixed, gram_mixed.T)
+    top_rows = jnp.concatenate([upper_left, upper_right], 1)
+    bottom_rows = jnp.concatenate([upper_right.T, lower_right], 1)
+    return jnp.concatenate([top_rows, bottom_rows], 0)
+
+
+def jacobi_kernel(low_ref, packed_ref, rotation_ref):
     highest = lax.Precision.HIGHEST
-    order_dim = gram_ref.shape[0]
+    gram = packed_gram(low_ref[0] != 0, packed_ref[...])
+    order_dim = gram.shape[0]
     last_idx = order_dim - 1
     width = order_dim // 2
-    gram = gram_ref[...]
     row_col = lax.broadcasted_iota(jnp.int32, (order_dim, 1), 0)
     row_full = lax.broadcasted_iota(jnp.int32, (order_dim, order_dim), 0)
     col_full = lax.broadcasted_iota(jnp.int32, (order_dim, order_dim), 1)
@@ -67,13 +85,14 @@
         )
     rotation_ref[...] = rotation
 
-def jacobi_pallas(gram):
+def jacobi_pallas(low, packed):
+    order_dim = 2 * packed.shape[1]
     return pl.pallas_call(
         jacobi_kernel,
-        out_shape=jax.ShapeDtypeStruct(gram.shape, jnp.float32),
-        in_specs=[pl.BlockSpec(memory_space=pltpu.VMEM)],
+        out_shape=jax.ShapeDtypeStruct((order_dim, order_dim), jnp.float32),
+        in_specs=[pl.BlockSpec(memory_space=pltpu.SMEM), pl.BlockSpec(memory_space=pltpu.VMEM)],
         out_specs=pl.BlockSpec(memory_space=pltpu.VMEM),
-    )(gram)
+    )(low, packed)
 
 
 def gram_kernel(mine_ref, theirs_ref, out_ref, acc_ref):
@@ -365,8 +384,7 @@
     own_low = column < partner
     branches = [functools.partial(exchange, bit_pos) for bit_pos in range(bit_count)]
     own_parts, other_parts, terms = lax.switch(bit_index, branches, snapshots)
-    gram_full = assemble(terms, own_low)
-    rotation = jacobi_pallas(gram_full)
+    rotation = jacobi_pallas(own_low.astype(jnp.int32).reshape(1), row_total(terms))
     width = own_parts.shape[0]
     own_columns = jnp.where(own_low, rotation[:, :width], rotation[:, width:])
     return rotate_part(own_columns, own_low, own_parts, other_parts)

time: 162 us -> 161 us (level)
  no operation moved by 1% of the time
where the time goes in v2:
time: 161 us
  blocking collectives  100 us (62%)
  Pallas kernels  34.2 us (21%)
  waiting for transfers between devices  16.4 us (10%)
  starting transfers between devices  3.82 us (2%)
  local copies, waits for them, and re-layouts  3.67 us (2%)
    all_to_all x1, blocking collectives, exchange(): lax.all_to_all(snapshots, 'rows', split_axis=1, concat_axis=0, tiled=True)  100 us
    pallas_call x2, Pallas kernels, split_terms(): pl.pallas_call(kernel, out_shape=jax.ShapeDtypeStruct((2 * width + 8, wid...  14.5 us
    ppermute x3, waiting for transfers between devices, row_total(): part = part + lax.ppermute(part, 'rows', pairs)  14.4 us
    pallas_call x1, Pallas kernels, jacobi_pallas(): pl.pallas_call(jacobi_kernel, out_shape=jax.ShapeDtypeStruct((order_dim,...  11.8 us
    pallas_call x1, Pallas kernels, rotate_part(): pl.pallas_call(rotate_kernel, out_shape=jax.ShapeDtypeStruct((width, cell...  7.9 us
    ppermute x3, starting transfers between devices, row_total(): part = part + lax.ppermute(part, 'rows', pairs)  3.82 us
  transfers between devices with their start and end apart: 4, of which 4 were waited for; matrix products, arithmetic and copies ran while one was open for 0% of the time, Pallas kernels for 3%

profile of v2, /device:TPU:0, one launch (start us, length us, event | category | flops | bytes accessed | tf_op | source)
XLA Modules:
  0.0 160.8 jit_solution(11925797790231979252)
XLA Ops:
  0.7 0.0 copy-start.5
  0.7 119.5 %conditional.1 = (f32[128,8192]{1,0:T(8,128)}, f32[128,8192]{1,0:T(8,128)}, f32[264,128]{1,0:T(8,128)S(1)}, f32[264,128]{1,0:T(8,128)S(1)}) conditional(s32[]{:T(128)} %clamp.3, f32[16,65536]{1,0:T(8,128)} %param.4, f32[16,65536]{1,0:T(8,128)} %param.4), branch_computations={%region_0.0_spmd, %region_1.0_spmd} | conditional | flops 1073809408 | bytes 77119960 | solution.py:386
  0.7 2.5 %copy.18 = f32[2,8,8,8192]{3,2,0,1:T(8,128)S(1)} copy(f32[2,8,8,8192]{3,2,1,0:T(8,128)} %bitcast.16) | data formatting | bytes 8388608 | tf_op jit(solution)/shard_map/cond/branch_0_fun/all_to_all | solution.py:293
  3.2 100.4 %all_to_all.31 = f32[16,8,8192]{2,0,1:T(8,128)} all-to-all(f32[16,8,8192]{2,0,1:T(8,128)S(1)} %bitcast.17), channel_id=1, replica_groups=mesh['rows'=8,'cols'=4] {'rows'}, dimensions={1} | all-to-all | bytes 8388608 | tf_op jit(solution)/shard_map/cond/branch_0_fun/all_to_all | solution.py:293
  103.5 0.0 collective-permute-start
  103.5 5.5 %branch_0_fun.2 = f32[264,128]{1,0:T(8,128)S(1)} custom-call(f32[128,8192]{1,0:T(8,128)} %bitcast.1.mine_ref), custom_call_target="tpu_custom_call" | custom-call | flops 268435456 | bytes 4194304 | tf_op jit(solution)/shard_map/cond/branch_0_fun/pallas_call | solution.py:211
  109.1 1.9 %collective-permute-done.theirs_ref = f32[128,8192]{1,0:T(8,128)} collective-permute-done((f32[128,8192]{1,0:T(8,128)}, f32[128,8192]{1,0:T(8,128)}, u32[]{:S(2)}, u32[]{:S(2)}) %collective-permute-start) | collective-permute-done | bytes 4194336 | tf_op jit(solution)/shard_map/cond/branch_0_fun/ppermute | solution.py:17
  111.0 8.9 %branch_0_fun.3 = f32[264,128]{1,0:T(8,128)S(1)} custom-call(f32[128,8192]{1,0:T(8,128)} %bitcast.1.mine_ref, f32[128,8192]{1,0:T(8,128)} %collective-permute-done.theirs_ref), custom_call_target="tpu_custom_call" | custom-call | flops 536870912 | bytes 8388608 | tf_op jit(solution)/shard_map/cond/branch_0_fun/pallas_call | solution.py:211
  120.2 1.5 collective-permute-start.5
  121.7 4.2 %collective-permute-done.5 = f32[264,128]{1,0:T(8,128)S(1)} collective-permute-done((f32[264,128]{1,0:T(8,128)S(1)}, f32[264,128]{1,0:T(8,128)S(1)}, u32[]{:S(2)}, u32[]{:S(2)}) %collective-permute-start.5) | collective-permute-done | bytes 135200 | tf_op jit(solution)/shard_map/ppermute | solution.py:248
  125.9 1.2 collective-permute-start.6
  127.1 3.9 %collective-permute-done.6 = f32[264,128]{1,0:T(8,128)S(1)} collective-permute-done((f32[264,128]{1,0:T(8,128)S(1)}, f32[264,128]{1,0:T(8,128)S(1)}, u32[]{:S(2)}, u32[]{:S(2)}) %collective-permute-start.6) | collective-permute-done | bytes 135200 | tf_op jit(solution)/shard_map/ppermute | solution.py:248
  131.0 1.1 collective-permute-start.7
  132.1 0.0 copy-done.5
  132.2 6.3 %collective-permute-done.7 = f32[264,128]{1,0:T(8,128)S(1)} collective-permute-done((f32[264,128]{1,0:T(8,128)S(1)}, f32[264,128]{1,0:T(8,128)S(1)}, u32[]{:S(2)}, u32[]{:S(2)}) %collective-permute-start.7) | collective-permute-done | bytes 135200 | tf_op jit(solution)/shard_map/ppermute | solution.py:248
  138.5 0.7 add.23.packed_ref
  139.2 11.8 %shard_map.34 = f32[256,256]{1,0:T(8,128)} custom-call(s32[1]{0:T(128)} %bitcast.8.low_ref, f32[264,128]{1,0:T(8,128)} %add.23.packed_ref), custom_call_target="tpu_custom_call" | custom-call | tf_op jit(solution)/shard_map/pallas_call | solution.py:90
  151.0 1.0 fusion
  152.0 0.1 copy.14
  152.1 0.1 copy.15
  152.3 0.7 maximum_bitcast_fusion.coef_ref
  152.9 7.9 %shard_map.35 = f32[128,8192]{1,0:T(8,128)} custom-call(f32[128,256]{1,0:T(8,128)} %maximum_bitcast_fusion.coef_ref, f32[128,8192]{1,0:T(8,128)} %get-tuple-element.40.mine_ref, f32[128,8192]{1,0:T(8,128)} %get-tuple-element.41.theirs_ref), custom_call_target="tpu_custom_call" | custom-call | flops 536870912 | bytes 12582912 | tf_op jit(solution)/shard_map/pallas_call | solution.py:364
  (5 shorter events, 0.1 us)
Async XLA Ops:
  0.7 131.5 %copy-start.5 = (s32[4]{0:T(128)S(1)}, s32[4]{0:T(128)}, u32[]{:S(2)}) copy-start(s32[4]{0:T(128)} %param.5) | copy-start | bytes 52
  103.5 7.5 %collective-permute-start = (f32[128,8192]{1,0:T(8,128)}, f32[128,8192]{1,0:T(8,128)}, u32[]{:S(2)}, u32[]{:S(2)}) collective-permute-start(f32[128,8192]{1,0:T(8,128)} %bitcast.1.mine_ref), channel_id=1, source_target_pairs={{0,1},{1,0},{2,3},{3,2},{4,5},{5,4},{6,7},{7,6},{8,9},{9,8},{10,11... | collective-permute-start | bytes 12582920 | tf_op jit(solution)/shard_map/cond/branch_0_fun/ppermute | solution.py:17
  120.2 5.7 %collective-permute-start.5 = (f32[264,128]{1,0:T(8,128)S(1)}, f32[264,128]{1,0:T(8,128)S(1)}, u32[]{:S(2)}, u32[]{:S(2)}) collective-permute-start(f32[264,128]{1,0:T(8,128)S(1)} %add.20), channel_id=1, source_target_pairs={{0,4},{4,0},{8,12},{12,8},{16,20},{20,16},{24,28},{28,24},{1,5},{5... | collective-permute-start | bytes 405512 | tf_op jit(solution)/shard_map/ppermute | solution.py:248
  125.9 5.1 %collective-permute-start.6 = (f32[264,128]{1,0:T(8,128)S(1)}, f32[264,128]{1,0:T(8,128)S(1)}, u32[]{:S(2)}, u32[]{:S(2)}) collective-permute-start(f32[264,128]{1,0:T(8,128)S(1)} %add.21), channel_id=1, source_target_pairs={{0,8},{4,12},{8,0},{12,4},{16,24},{20,28},{24,16},{28,20},{1,9},{5... | collective-permute-start | bytes 405512 | tf_op jit(solution)/shard_map/ppermute | solution.py:248
  131.0 7.5 %collective-permute-start.7 = (f32[264,128]{1,0:T(8,128)S(1)}, f32[264,128]{1,0:T(8,128)S(1)}, u32[]{:S(2)}, u32[]{:S(2)}) collective-permute-start(f32[264,128]{1,0:T(8,128)S(1)} %add.22), channel_id=1, source_target_pairs={{0,16},{4,20},{8,24},{12,28},{16,0},{20,4},{24,8},{28,12},{1,17},{... | collective-permute-start | bytes 405512 | tf_op jit(solution)/shard_map/ppermute | solution.py:248

commit v3 on v2

--- a/solution.py
+++ b/solution.py
@@ -346,31 +346,39 @@
     return jnp.concatenate([top_rows, bottom_rows], 0)
 
 
-def rotate_kernel(coef_ref, mine_ref, theirs_ref, out_ref):
+def rotate_kernel(low_ref, rotation_ref, mine_ref, theirs_ref, out_ref):
+    low = low_ref[0] != 0
+    rotation = rotation_ref[...]
+    width = mine_ref.shape[0]
+    own_columns = jnp.where(low, rotation[:, :width], rotation[:, width:])
+    coef_mine = jnp.where(low, own_columns[:width], own_columns[width:])
+    coef_theirs = jnp.where(low, own_columns[width:], own_columns[:width])
+    coef = jnp.concatenate([coef_mine, coef_theirs], 0).T
     stacked = jnp.concatenate([mine_ref[...], theirs_ref[...]], 0)
     out_ref[...] = jnp.dot(
-        coef_ref[...], stacked, precision=lax.Precision.HIGHEST, preferred_element_type=jnp.float32
+        coef, stacked, precision=lax.Precision.HIGHEST, preferred_element_type=jnp.float32
     )
 
 
-def rotate_part(columns_sel, own_low, mine, theirs):
+def rotate_part(rotation, low, mine, theirs):
     width, cells = mine.shape
-    coef_mine = jnp.where(own_low, columns_sel[:width], columns_sel[width:])
-    coef_theirs = jnp.where(own_low, columns_sel[width:], columns_sel[:width])
-    coef = jnp.concatenate([coef_mine, coef_theirs], 0).T
     tile = min(cells, 2048)
-    coef_spec = pl.BlockSpec((width, 2 * width), lambda step: (0, 0))
     cell_spec = pl.BlockSpec((width, tile), lambda step: (0, step))
     return pl.pallas_call(
         rotate_kernel,
         out_shape=jax.ShapeDtypeStruct((width, cells), jnp.float32),
         grid=(cells // tile,),
-        in_specs=[coef_spec, cell_spec, cell_spec],
+        in_specs=[
+            pl.BlockSpec(memory_space=pltpu.SMEM),
+            pl.BlockSpec(rotation.shape, lambda step: (0, 0)),
+            cell_spec,
+            cell_spec,
+        ],
         out_specs=cell_spec,
         cost_estimate=pl.CostEstimate(
             flops=4 * width * width * cells, transcendentals=0, bytes_accessed=12 * width * cells
         ),
-    )(coef, mine, theirs)
+    )(low, rotation, mine, theirs)
 
 
 def shards(snapshots, pair_table):
@@ -384,10 +392,9 @@
     own_low = column < partner
     branches = [functools.partial(exchange, bit_pos) for bit_pos in range(bit_count)]
     own_parts, other_parts, terms = lax.switch(bit_index, branches, snapshots)
-    rotation = jacobi_pallas(own_low.astype(jnp.int32).reshape(1), row_total(terms))
-    width = own_parts.shape[0]
-    own_columns = jnp.where(own_low, rotation[:, :width], rotation[:, width:])
-    return rotate_part(own_columns, own_low, own_parts, other_parts)
+    low = own_low.astype(jnp.int32).reshape(1)
+    rotation = jacobi_pallas(low, row_total(terms))
+    return rotate_part(rotation, low, own_parts, other_parts)
 
 
 def solution(mesh):

time: 161 us -> 159 us (0.988)
  no operation moved by 1% of the time
where the time goes in v3:
time: 159 us
  blocking collectives  100 us (63%)
  Pallas kernels  34.3 us (22%)
  waiting for transfers between devices  16.4 us (10%)
  starting transfers between devices  3.82 us (2%)
  local copies, waits for them, and re-layouts  2.49 us (2%)
    all_to_all x1, blocking collectives, exchange(): lax.all_to_all(snapshots, 'rows', split_axis=1, concat_axis=0, tiled=True)  100 us
    pallas_call x2, Pallas kernels, split_terms(): pl.pallas_call(kernel, out_shape=jax.ShapeDtypeStruct((2 * width + 8, wid...  14.5 us
    ppermute x3, waiting for transfers between devices, row_total(): part = part + lax.ppermute(part, 'rows', pairs)  14.4 us
    pallas_call x1, Pallas kernels, jacobi_pallas(): pl.pallas_call(jacobi_kernel, out_shape=jax.ShapeDtypeStruct((order_dim,...  11.8 us
    pallas_call x1, Pallas kernels, rotate_part(): pl.pallas_call(rotate_kernel, out_shape=jax.ShapeDtypeStruct((width, cell...  8.02 us
    ppermute x3, starting transfers between devices, row_total(): part = part + lax.ppermute(part, 'rows', pairs)  3.82 us
  transfers between devices with their start and end apart: 4, of which 4 were waited for; matrix products, arithmetic and copies ran while one was open for 0% of the time, Pallas kernels for 3%

profile of v3, /device:TPU:0, one launch (start us, length us, event | category | flops | bytes accessed | tf_op | source)
XLA Modules:
  0.0 159.1 jit_solution(9299593905585438252)
XLA Ops:
  0.7 0.0 copy-start.5
  0.7 119.5 %conditional.1 = (f32[128,8192]{1,0:T(8,128)}, f32[128,8192]{1,0:T(8,128)}, f32[264,128]{1,0:T(8,128)S(1)}, f32[264,128]{1,0:T(8,128)S(1)}) conditional(s32[]{:T(128)} %clamp.3, f32[16,65536]{1,0:T(8,128)} %param.4, f32[16,65536]{1,0:T(8,128)} %param.4), branch_computations={%region_0.0_spmd, %region_1.0_spmd} | conditional | flops 1073809408 | bytes 77119960 | solution.py:394
  0.7 2.5 %copy.14 = f32[2,8,8,8192]{3,2,0,1:T(8,128)S(1)} copy(f32[2,8,8,8192]{3,2,1,0:T(8,128)} %bitcast.14) | data formatting | bytes 8388608 | tf_op jit(solution)/shard_map/cond/branch_0_fun/all_to_all | solution.py:293
  3.2 100.4 %all_to_all.31 = f32[16,8,8192]{2,0,1:T(8,128)} all-to-all(f32[16,8,8192]{2,0,1:T(8,128)S(1)} %bitcast.15), channel_id=1, replica_groups=mesh['rows'=8,'cols'=4] {'rows'}, dimensions={1} | all-to-all | bytes 8388608 | tf_op jit(solution)/shard_map/cond/branch_0_fun/all_to_all | solution.py:293
  103.5 0.0 collective-permute-start
  103.5 5.5 %branch_0_fun.2 = f32[264,128]{1,0:T(8,128)S(1)} custom-call(f32[128,8192]{1,0:T(8,128)} %bitcast.1.mine_ref), custom_call_target="tpu_custom_call" | custom-call | flops 268435456 | bytes 4194304 | tf_op jit(solution)/shard_map/cond/branch_0_fun/pallas_call | solution.py:211
  109.1 1.9 %collective-permute-done.theirs_ref = f32[128,8192]{1,0:T(8,128)} collective-permute-done((f32[128,8192]{1,0:T(8,128)}, f32[128,8192]{1,0:T(8,128)}, u32[]{:S(2)}, u32[]{:S(2)}) %collective-permute-start) | collective-permute-done | bytes 4194336 | tf_op jit(solution)/shard_map/cond/branch_0_fun/ppermute | solution.py:17
  111.0 8.9 %branch_0_fun.3 = f32[264,128]{1,0:T(8,128)S(1)} custom-call(f32[128,8192]{1,0:T(8,128)} %bitcast.1.mine_ref, f32[128,8192]{1,0:T(8,128)} %collective-permute-done.theirs_ref), custom_call_target="tpu_custom_call" | custom-call | flops 536870912 | bytes 8388608 | tf_op jit(solution)/shard_map/cond/branch_0_fun/pallas_call | solution.py:211
  120.2 1.5 collective-permute-start.5
  121.7 4.2 %collective-permute-done.5 = f32[264,128]{1,0:T(8,128)S(1)} collective-permute-done((f32[264,128]{1,0:T(8,128)S(1)}, f32[264,128]{1,0:T(8,128)S(1)}, u32[]{:S(2)}, u32[]{:S(2)}) %collective-permute-start.5) | collective-permute-done | bytes 135200 | tf_op jit(solution)/shard_map/ppermute | solution.py:248
  125.9 1.2 collective-permute-start.6
  127.1 3.9 %collective-permute-done.6 = f32[264,128]{1,0:T(8,128)S(1)} collective-permute-done((f32[264,128]{1,0:T(8,128)S(1)}, f32[264,128]{1,0:T(8,128)S(1)}, u32[]{:S(2)}, u32[]{:S(2)}) %collective-permute-start.6) | collective-permute-done | bytes 135200 | tf_op jit(solution)/shard_map/ppermute | solution.py:248
  131.0 1.1 collective-permute-start.7
  132.1 0.0 copy-done.5
  132.2 6.3 %collective-permute-done.7 = f32[264,128]{1,0:T(8,128)S(1)} collective-permute-done((f32[264,128]{1,0:T(8,128)S(1)}, f32[264,128]{1,0:T(8,128)S(1)}, u32[]{:S(2)}, u32[]{:S(2)}) %collective-permute-start.7) | collective-permute-done | bytes 135200 | tf_op jit(solution)/shard_map/ppermute | solution.py:248
  138.5 0.7 add.23.packed_ref
  139.2 11.8 %shard_map.34.rotation_ref = f32[256,256]{1,0:T(8,128)} custom-call(s32[1]{0:T(128)} %bitcast.8.low_ref, f32[264,128]{1,0:T(8,128)} %add.23.packed_ref), custom_call_target="tpu_custom_call" | custom-call | tf_op jit(solution)/shard_map/pallas_call | solution.py:90
  151.1 8.0 %shard_map.35 = f32[128,8192]{1,0:T(8,128)} custom-call(s32[1]{0:T(128)} %bitcast.8.low_ref, f32[256,256]{1,0:T(8,128)} %shard_map.34.rotation_ref, f32[128,8192]{1,0:T(8,128)} %get-tuple-element.40.mine_ref, f32[128,8192]{1,0:T(8,128)} %get-tuple-element.41.theirs_ref), custom_call_target="tpu_custom_call" | custom-call | flops 536870912 | bytes 12582912 | tf_op jit(solution)/shard_map/pallas_call | solution.py:367
  (3 shorter events, 0.1 us)
Async XLA Ops:
  0.7 131.5 %copy-start.5 = (s32[4]{0:T(128)S(1)}, s32[4]{0:T(128)}, u32[]{:S(2)}) copy-start(s32[4]{0:T(128)} %param.5) | copy-start | bytes 52
  103.5 7.5 %collective-permute-start = (f32[128,8192]{1,0:T(8,128)}, f32[128,8192]{1,0:T(8,128)}, u32[]{:S(2)}, u32[]{:S(2)}) collective-permute-start(f32[128,8192]{1,0:T(8,128)} %bitcast.1.mine_ref), channel_id=1, source_target_pairs={{0,1},{1,0},{2,3},{3,2},{4,5},{5,4},{6,7},{7,6},{8,9},{9,8},{10,11... | collective-permute-start | bytes 12582920 | tf_op jit(solution)/shard_map/cond/branch_0_fun/ppermute | solution.py:17
  120.2 5.7 %collective-permute-start.5 = (f32[264,128]{1,0:T(8,128)S(1)}, f32[264,128]{1,0:T(8,128)S(1)}, u32[]{:S(2)}, u32[]{:S(2)}) collective-permute-start(f32[264,128]{1,0:T(8,128)S(1)} %add.20), channel_id=1, source_target_pairs={{0,4},{4,0},{8,12},{12,8},{16,20},{20,16},{24,28},{28,24},{1,5},{5... | collective-permute-start | bytes 405512 | tf_op jit(solution)/shard_map/ppermute | solution.py:248
  125.9 5.1 %collective-permute-start.6 = (f32[264,128]{1,0:T(8,128)S(1)}, f32[264,128]{1,0:T(8,128)S(1)}, u32[]{:S(2)}, u32[]{:S(2)}) collective-permute-start(f32[264,128]{1,0:T(8,128)S(1)} %add.21), channel_id=1, source_target_pairs={{0,8},{4,12},{8,0},{12,4},{16,24},{20,28},{24,16},{28,20},{1,9},{5... | collective-permute-start | bytes 405512 | tf_op jit(solution)/shard_map/ppermute | solution.py:248
  131.0 7.5 %collective-permute-start.7 = (f32[264,128]{1,0:T(8,128)S(1)}, f32[264,128]{1,0:T(8,128)S(1)}, u32[]{:S(2)}, u32[]{:S(2)}) collective-permute-start(f32[264,128]{1,0:T(8,128)S(1)} %add.22), channel_id=1, source_target_pairs={{0,16},{4,20},{8,24},{12,28},{16,0},{20,4},{24,8},{28,12},{1,17},{... | collective-permute-start | bytes 405512 | tf_op jit(solution)/shard_map/ppermute | solution.py:248

commit v4 on v3

--- a/solution.py
+++ b/solution.py
@@ -123,14 +123,17 @@
         out_ref[2 * width :, :] = jnp.broadcast_to(diag_theirs, (8, width))
 
 
-def gram_store_kernel(mine_ref, theirs_ref, own_in, other_in, out_ref, own_ref, other_ref, acc_ref):
+def gram_store_kernel(
+    mine_ref, theirs_ref, own_in, other_in, terms_in, out_ref, own_ref, other_ref, acc_ref
+):
     del own_in, other_in
     gram_kernel(mine_ref, theirs_ref, out_ref, acc_ref)
+    out_ref[...] = out_ref[...] + terms_in[...]
     own_ref[...] = mine_ref[...]
     other_ref[...] = theirs_ref[...]
 
 
-def pair_terms_stored(mine, theirs, own_full, other_full, chunk):
+def pair_terms_stored(mine, theirs, own_full, other_full, terms, chunk):
     width, piece = mine.shape
     cell_spec = pl.BlockSpec((width, piece), lambda step: (0, 0))
     full_spec = pl.BlockSpec((width, piece), lambda step: (0, chunk))
@@ -142,14 +145,20 @@
             jax.ShapeDtypeStruct(other_full.shape, other_full.dtype),
         ],
         grid=(1,),
-        in_specs=[cell_spec, cell_spec, pl.BlockSpec(memory_space=pl.ANY), pl.BlockSpec(memory_space=pl.ANY)],
+        in_specs=[
+            cell_spec,
+            cell_spec,
+            pl.BlockSpec(memory_space=pl.ANY),
+            pl.BlockSpec(memory_space=pl.ANY),
+            pl.BlockSpec((2 * width + 8, width), lambda step: (0, 0)),
+        ],
         out_specs=[pl.BlockSpec((2 * width + 8, width), lambda step: (0, 0)), full_spec, full_spec],
         scratch_shapes=[pltpu.VMEM((2 * width, 2 * width), jnp.float32)],
-        input_output_aliases={2: 1, 3: 2},
+        input_output_aliases={2: 1, 3: 2, 4: 0},
         cost_estimate=pl.CostEstimate(
             flops=8 * width * width * piece, transcendentals=0, bytes_accessed=16 * width * piece
         ),
-    )(mine, theirs, own_full, other_full)
+    )(mine, theirs, own_full, other_full, terms)
 
 
 def mine_kernel(mine_ref, out_ref, acc_ref):
@@ -318,10 +327,10 @@
     other_parts.append(partner_2(own_parts[-1], "cols", bit_pos))
     own_full = jnp.zeros((rows_n * local_rows, width), snapshots.dtype)
     other_full = jnp.zeros((rows_n * local_rows, width), snapshots.dtype)
-    terms = None
+    width_rows = rows_n * local_rows
+    terms = jnp.zeros((2 * width_rows + 8, width_rows), jnp.float32)
     for chunk, (mine, theirs) in enumerate(zip(own_parts, other_parts)):
-        part, own_full, other_full = pair_terms_stored(mine, theirs, own_full, other_full, chunk)
-        terms = part if terms is None else terms + part
+        terms, own_full, other_full = pair_terms_stored(mine, theirs, own_full, other_full, terms, chunk)
     return own_full, other_full, terms
 
 

time: 159 us -> 196 us (1.23)
  blocking collectives: 100 us -> 0 us
  waiting for transfers between devices: 16.4 us -> 108 us
  starting transfers between devices: 3.82 us -> 28.8 us
  Pallas kernels: 34.3 us -> 50.5 us
  local copies, waits for them, and re-layouts: 2.49 us -> 5.52 us
    all_to_all x1 -> x0, blocking collectives: 100 us -> none  [exchange(): lax.all_to_all(snapshots, 'rows', split_axis=1, concat_axis=0, tiled=True)]
    ppermute x1 -> x4, waiting for transfers between devices: 1.95 us -> 47.4 us  [partner_2(): return lax.ppermute(value, axis, pairs)]
    all_to_all x0 -> x4, waiting for transfers between devices: none -> 45.4 us  [spread(): got = lax.all_to_all(sent, 'rows', split_axis=0, concat_axis=0)]
    all_to_all x0 -> x4, starting transfers between devices: none -> 20 us  [spread(): got = lax.all_to_all(sent, 'rows', split_axis=0, concat_axis=0)]
    pallas_call x2 -> x6, Pallas kernels: 14.5 us -> 30.7 us  [the longest x4 19.2 us: pair_terms_stored(): pl.pallas_call(gram_store_kernel, out_shape=[jax.ShapeDtypeStruct((2 * wi...]
    ppermute x1 -> x4, starting transfers between devices: 0.01 us -> 6.07 us  [partner_2(): return lax.ppermute(value, axis, pairs)]
    another operation x0 -> x3, local copies, waits for them, and re-layouts: none -> 5.5 us
    all_to_all x1 -> x0, local copies, waits for them, and re-layouts: 2.49 us -> none  [exchange(): lax.all_to_all(snapshots, 'rows', split_axis=1, concat_axis=0, tiled=True)]
  transfers between devices with their start and end apart: 4 -> 11, of which waited for: 4 -> 10; matrix products, arithmetic and copies ran while one was open for 0% -> 3% of each run, Pallas kernels for 3% -> 11%
where the time goes in v4:
time: 196 us
  waiting for transfers between devices  108 us (55%)
  Pallas kernels  50.5 us (26%)
  starting transfers between devices  28.8 us (15%)
  local copies, waits for them, and re-layouts  5.52 us (3%)
    ppermute x4, waiting for transfers between devices, partner_2(): return lax.ppermute(value, axis, pairs)  47.4 us
    all_to_all x4, waiting for transfers between devices, spread(): got = lax.all_to_all(sent, 'rows', split_axis=0, concat_axis=0)  45.4 us
    all_to_all x4, starting transfers between devices, spread(): got = lax.all_to_all(sent, 'rows', split_axis=0, concat_axis=0)  20 us
    pallas_call x4, Pallas kernels, pair_terms_stored(): pl.pallas_call(gram_store_kernel, out_shape=[jax.ShapeDtypeStruct((2 * wi...  19.2 us
    ppermute x3, waiting for transfers between devices, row_total(): part = part + lax.ppermute(part, 'rows', pairs)  15.4 us
    pallas_call x1, Pallas kernels, jacobi_pallas(): pl.pallas_call(jacobi_kernel, out_shape=jax.ShapeDtypeStruct((order_dim,...  11.8 us
    pallas_call x2, Pallas kernels, lay_out(): pl.pallas_call(functools.partial(lay_kernel, tuple(chunk_ids), piece), ou...  11.5 us
    pallas_call x1, Pallas kernels, rotate_part(): pl.pallas_call(rotate_kernel, out_shape=jax.ShapeDtypeStruct((width, cell...  8.02 us
  transfers between devices with their start and end apart: 11, of which 10 were waited for; matrix products, arithmetic and copies ran while one was open for 3% of the time, Pallas kernels for 11%

profile of v4, /device:TPU:0, one launch (start us, length us, event | category | flops | bytes accessed | tf_op | source)
XLA Modules:
  0.0 195.5 jit_solution(10669043553537513310)
XLA Ops:
  0.7 155.1 %conditional.1 = (f32[128,8192]{1,0:T(8,128)}, f32[128,8192]{1,0:T(8,128)}, f32[264,128]{1,0:T(8,128)}) conditional(s32[]{:T(128)} %clamp.3, f32[16,65536]{1,0:T(8,128)} %param.4, f32[16,65536]{1,0:T(8,128)} %param.4), branch_computations={%region_0.0_spmd, %region_1.0_spmd} | conditional | flops 1073741824 | bytes 75633048 | solution.py:403
  0.7 5.2 %branch_1_fun.6 = f32[8,16,2048]{2,1,0:T(8,128)} custom-call(f32[16,65536]{1,0:T(8,128)} %source_ref.1), custom_call_target="tpu_custom_call" | custom-call | bytes 2097152 | tf_op jit(solution)/shard_map/cond/branch_1_fun/pallas_call | solution.py:278
  5.9 7.3 %all-to-all-start = ((f32[8,16,2048]{2,1,0:T(8,128)}), f32[8,16,2048]{2,1,0:T(8,128)S(1)}, u32[]{:S(2)}, u32[]{:S(2)}) async-start(f32[8,16,2048]{2,1,0:T(8,128)} %branch_1_fun.6), calls=%async_computation | async-start | bytes 2097152 | tf_op jit(solution)/shard_map/cond/branch_1_fun/all_to_all | solution.py:314
  13.2 6.3 %branch_1_fun.7 = (f32[8,16,2048]{2,1,0:T(8,128)}, f32[8,16,2048]{2,1,0:T(8,128)}, f32[8,16,2048]{2,1,0:T(8,128)}) custom-call(f32[16,65536]{1,0:T(8,128)} %source_ref.1), custom_call_target="tpu_custom_call" | custom-call | bytes 6291456 | tf_op jit(solution)/shard_map/cond/branch_1_fun/pallas_call | solution.py:278
  19.5 19.5 %all-to-all-done = f32[8,16,2048]{2,1,0:T(8,128)S(1)} async-done(((f32[8,16,2048]{2,1,0:T(8,128)}), f32[8,16,2048]{2,1,0:T(8,128)S(1)}, u32[]{:S(2)}, u32[]{:S(2)}) %all-to-all-start) | async-done | bytes 1048608 | tf_op jit(solution)/shard_map/cond/branch_1_fun/all_to_all | solution.py:314
  38.9 3.6 %all-to-all-start.1 = ((f32[8,16,2048]{2,1,0:T(8,128)}), f32[8,16,2048]{2,1,0:T(8,128)S(1)}, u32[]{:S(2)}, u32[]{:S(2)}) async-start(f32[8,16,2048]{2,1,0:T(8,128)} %get-tuple-element.8), calls=%async_computation.1 | async-start | bytes 2097152 | tf_op jit(solution)/shard_map/cond/branch_1_fun/all_to_all | solution.py:314
  44.1 23.4 %collective-permute-done.theirs_ref = f32[128,2048]{1,0:T(8,128)} collective-permute-done((f32[128,2048]{1,0:T(8,128)S(1)}, f32[128,2048]{1,0:T(8,128)}, u32[]{:S(2)}, u32[]{:S(2)}) %collective-permute-start) | collective-permute-done | bytes 1048608 | tf_op jit(solution)/shard_map/cond/branch_1_fun/ppermute | solution.py:17
  68.5 4.7 %all-to-all-start.2 = ((f32[8,16,2048]{2,1,0:T(8,128)}), f32[8,16,2048]{2,1,0:T(8,128)S(1)}, u32[]{:S(2)}, u32[]{:S(2)}) async-start(f32[8,16,2048]{2,1,0:T(8,128)} %get-tuple-element.11), calls=%async_computation.2 | async-start | bytes 2097152 | tf_op jit(solution)/shard_map/cond/branch_1_fun/all_to_all | solution.py:314
  74.7 22.4 %collective-permute-done.1.theirs_ref = f32[128,2048]{1,0:T(8,128)} collective-permute-done((f32[128,2048]{1,0:T(8,128)S(1)}, f32[128,2048]{1,0:T(8,128)}, u32[]{:S(2)}, u32[]{:S(2)}) %collective-permute-start.1) | collective-permute-done | bytes 1048608 | tf_op jit(solution)/shard_map/cond/branch_1_fun/ppermute | solution.py:17
  98.3 4.5 %all-to-all-start.3 = ((f32[8,16,2048]{2,1,0:T(8,128)}), f32[8,16,2048]{2,1,0:T(8,128)}, u32[]{:S(2)}, u32[]{:S(2)}) async-start(f32[8,16,2048]{2,1,0:T(8,128)} %get-tuple-element.14), calls=%async_computation.3 | async-start | bytes 2097152 | tf_op jit(solution)/shard_map/cond/branch_1_fun/all_to_all | solution.py:314
  104.3 23.6 %all-to-all-done.3 = f32[8,16,2048]{2,1,0:T(8,128)} async-done(((f32[8,16,2048]{2,1,0:T(8,128)}), f32[8,16,2048]{2,1,0:T(8,128)}, u32[]{:S(2)}, u32[]{:S(2)}) %all-to-all-start.3) | async-done | bytes 1048608 | tf_op jit(solution)/shard_map/cond/branch_1_fun/all_to_all | solution.py:314
  129.4 2.4 %broadcast_3_own_in_other_in.0.own_in = f32[128,8192]{1,0:T(8,128)} broadcast(f32[]{:T(128)} %constant.4.clone), dimensions={} | broadcast | bytes 4194308 | tf_op jit(solution)/shard_map/broadcast.3.own_in.other_in
  131.8 2.5 %broadcast_3_own_in_other_in.0.clone.other_in = f32[128,8192]{1,0:T(8,128)} broadcast(f32[]{:T(128)} %constant.4.clone), dimensions={} | broadcast | bytes 4194308 | tf_op jit(solution)/shard_map/broadcast.3.own_in.other_in
  134.9 4.8 %branch_1_fun.8 = (f32[264,128]{1,0:T(8,128)}, f32[128,8192]{1,0:T(8,128)}, f32[128,8192]{1,0:T(8,128)}) custom-call(f32[128,2048]{1,0:T(8,128)} %bitcast.17, f32[128,2048]{1,0:T(8,128)} %collective-permute-done.theirs_ref, f32[128,8192]{1,0:T(8,128)} %broadcast_3_own_in_other_in.0.own_in, ...), custom_call_target="tpu_custom_call", output_to_operand_aliasing={{1}: (2, {}), {2}: (3, {}), {0}: (4, {})} | custom-call | flops 268435456 | bytes 4194304 | tf_op jit(solution)/shard_map/cond/branch_1_fun/pallas_call | solution.py:140
  139.7 4.8 %branch_1_fun.9 = (f32[264,128]{1,0:T(8,128)}, f32[128,8192]{1,0:T(8,128)}, f32[128,8192]{1,0:T(8,128)}) custom-call(f32[128,2048]{1,0:T(8,128)} %bitcast.19, f32[128,2048]{1,0:T(8,128)} %collective-permute-done.1.theirs_ref, f32[128,8192]{1,0:T(8,128)} %get-tuple-element.18.own_in, ...), custom_call_target="tpu_custom_call", output_to_operand_aliasing={{1}: (2, {}), {2}: (3, {}), {0}: (4, {})} | custom-call | flops 268435456 | bytes 4194304 | tf_op jit(solution)/shard_map/cond/branch_1_fun/pallas_call | solution.py:140
  144.5 4.8 %branch_1_fun.10 = (f32[264,128]{1,0:T(8,128)}, f32[128,8192]{1,0:T(8,128)}, f32[128,8192]{1,0:T(8,128)}) custom-call(f32[128,2048]{1,0:T(8,128)} %bitcast.21, f32[128,2048]{1,0:T(8,128)} %collective-permute-done.3.theirs_ref, f32[128,8192]{1,0:T(8,128)} %get-tuple-element.21.own_in, ...), custom_call_target="tpu_custom_call", output_to_operand_aliasing={{1}: (2, {}), {2}: (3, {}), {0}: (4, {})} | custom-call | flops 268435456 | bytes 4194304 | tf_op jit(solution)/shard_map/cond/branch_1_fun/pallas_call | solution.py:140
  149.3 1.7 collective-permute-done.2.theirs_ref
  151.0 4.8 %branch_1_fun.11 = (f32[264,128]{1,0:T(8,128)}, f32[128,8192]{1,0:T(8,128)}, f32[128,8192]{1,0:T(8,128)}) custom-call(f32[128,2048]{1,0:T(8,128)} %bitcast.6.mine_ref, f32[128,2048]{1,0:T(8,128)} %collective-permute-done.2.theirs_ref, f32[128,8192]{1,0:T(8,128)} %get-tuple-element.24.own_in, ...), custom_call_target="tpu_custom_call", output_to_operand_aliasing={{1}: (2, {}), {2}: (3, {}), {0}: (4, {})} | custom-call | flops 268435456 | bytes 4194304 | tf_op jit(solution)/shard_map/cond/branch_1_fun/pallas_call | solution.py:140
  155.8 2.5 %collective-permute-start.5 = (f32[264,128]{1,0:T(8,128)}, f32[264,128]{1,0:T(8,128)S(1)}, u32[]{:S(2)}, u32[]{:S(2)}) collective-permute-start(f32[264,128]{1,0:T(8,128)} %get-tuple-element.33), channel_id=1, source_target_pairs={{0,4},{4,0},{8,12},{12,8},{16,20},{20,16},{24,28},{28,24},{1,5},{5... | collective-permute-start | bytes 405512 | tf_op jit(solution)/shard_map/ppermute | solution.py:257
  158.4 3.2 %collective-permute-done.5 = f32[264,128]{1,0:T(8,128)S(1)} collective-permute-done((f32[264,128]{1,0:T(8,128)}, f32[264,128]{1,0:T(8,128)S(1)}, u32[]{:S(2)}, u32[]{:S(2)}) %collective-permute-start.5) | collective-permute-done | bytes 135200 | tf_op jit(solution)/shard_map/ppermute | solution.py:257
  162.6 6.0 %collective-permute-done.6 = f32[264,128]{1,0:T(8,128)S(1)} collective-permute-done((f32[264,128]{1,0:T(8,128)S(1)}, f32[264,128]{1,0:T(8,128)S(1)}, u32[]{:S(2)}, u32[]{:S(2)}) %collective-permute-start.6) | collective-permute-done | bytes 135200 | tf_op jit(solution)/shard_map/ppermute | solution.py:257
  168.7 6.3 %collective-permute-done.7 = f32[264,128]{1,0:T(8,128)S(1)} collective-permute-done((f32[264,128]{1,0:T(8,128)S(1)}, f32[264,128]{1,0:T(8,128)S(1)}, u32[]{:S(2)}, u32[]{:S(2)}) %collective-permute-start.7) | collective-permute-done | bytes 135200 | tf_op jit(solution)/shard_map/ppermute | solution.py:257
  175.7 11.8 %shard_map.34.rotation_ref = f32[256,256]{1,0:T(8,128)} custom-call(s32[1]{0:T(128)} %bitcast.8.low_ref, f32[264,128]{1,0:T(8,128)} %add.14.packed_ref), custom_call_target="tpu_custom_call" | custom-call | tf_op jit(solution)/shard_map/pallas_call | solution.py:90
  187.5 8.0 %shard_map.35 = f32[128,8192]{1,0:T(8,128)} custom-call(s32[1]{0:T(128)} %bitcast.8.low_ref, f32[256,256]{1,0:T(8,128)} %shard_map.34.rotation_ref, f32[128,8192]{1,0:T(8,128)} %get-tuple-element.34.mine_ref, f32[128,8192]{1,0:T(8,128)} %get-tuple-element.35.theirs_ref), custom_call_target="tpu_custom_call" | custom-call | flops 536870912 | bytes 12582912 | tf_op jit(solution)/shard_map/pallas_call | solution.py:376
  (21 shorter events, 10.8 us)
Async XLA Ops:
  0.7 168.0 %copy-start.4 = (s32[4]{0:T(128)S(1)}, s32[4]{0:T(128)}, u32[]{:S(2)}) copy-start(s32[4]{0:T(128)} %param.5) | copy-start | bytes 52
  5.9 33.0 %all-to-all-start = ((f32[8,16,2048]{2,1,0:T(8,128)}), f32[8,16,2048]{2,1,0:T(8,128)S(1)}, u32[]{:S(2)}, u32[]{:S(2)}) async-start(f32[8,16,2048]{2,1,0:T(8,128)} %branch_1_fun.6), calls=%async_computation | async-start | bytes 2097152 | tf_op jit(solution)/shard_map/cond/branch_1_fun/all_to_all | solution.py:314
  38.9 92.9 %copy-start = (f32[8,16,2048]{2,1,0:T(8,128)}, f32[8,16,2048]{2,1,0:T(8,128)S(1)}, u32[]{:S(2)}) copy-start(f32[8,16,2048]{2,1,0:T(8,128)S(1)} %all-to-all-done) | copy-start | bytes 3145732 | tf_op jit(solution)/shard_map/cond
  38.9 29.5 %all-to-all-start.1 = ((f32[8,16,2048]{2,1,0:T(8,128)}), f32[8,16,2048]{2,1,0:T(8,128)S(1)}, u32[]{:S(2)}, u32[]{:S(2)}) async-start(f32[8,16,2048]{2,1,0:T(8,128)} %get-tuple-element.8), calls=%async_computation.1 | async-start | bytes 2097152 | tf_op jit(solution)/shard_map/cond/branch_1_fun/all_to_all | solution.py:314
  42.5 24.9 %collective-permute-start = (f32[128,2048]{1,0:T(8,128)S(1)}, f32[128,2048]{1,0:T(8,128)}, u32[]{:S(2)}, u32[]{:S(2)}) collective-permute-start(f32[128,2048]{1,0:T(8,128)S(1)} %bitcast.16), channel_id=1, source_target_pairs={{0,2},{1,3},{2,0},{3,1},{4,6},{5,7},{6,4},{7,5},{8,10},{9,11},{10,... | collective-permute-start | bytes 3145736 | tf_op jit(solution)/shard_map/cond/branch_1_fun/ppermute | solution.py:17
  68.5 63.3 %copy-start.1 = (f32[8,16,2048]{2,1,0:T(8,128)}, f32[8,16,2048]{2,1,0:T(8,128)S(1)}, u32[]{:S(2)}) copy-start(f32[8,16,2048]{2,1,0:T(8,128)S(1)} %all-to-all-done.1) | copy-start | bytes 3145732 | tf_op jit(solution)/shard_map/cond
  68.5 29.8 %all-to-all-start.2 = ((f32[8,16,2048]{2,1,0:T(8,128)}), f32[8,16,2048]{2,1,0:T(8,128)S(1)}, u32[]{:S(2)}, u32[]{:S(2)}) async-start(f32[8,16,2048]{2,1,0:T(8,128)} %get-tuple-element.11), calls=%async_computation.2 | async-start | bytes 2097152 | tf_op jit(solution)/shard_map/cond/branch_1_fun/all_to_all | solution.py:314
  73.2 23.9 %collective-permute-start.1 = (f32[128,2048]{1,0:T(8,128)S(1)}, f32[128,2048]{1,0:T(8,128)}, u32[]{:S(2)}, u32[]{:S(2)}) collective-permute-start(f32[128,2048]{1,0:T(8,128)S(1)} %bitcast.18), channel_id=1, source_target_pairs={{0,2},{1,3},{2,0},{3,1},{4,6},{5,7},{6,4},{7,5},{8,10},{9,11},{10,... | collective-permute-start | bytes 3145736 | tf_op jit(solution)/shard_map/cond/branch_1_fun/ppermute | solution.py:17
  98.3 36.0 %copy-start.2 = (f32[8,16,2048]{2,1,0:T(8,128)}, f32[8,16,2048]{2,1,0:T(8,128)S(1)}, u32[]{:S(2)}) copy-start(f32[8,16,2048]{2,1,0:T(8,128)S(1)} %all-to-all-done.2) | copy-start | bytes 3145732 | tf_op jit(solution)/shard_map/cond
  98.3 29.6 %all-to-all-start.3 = ((f32[8,16,2048]{2,1,0:T(8,128)}), f32[8,16,2048]{2,1,0:T(8,128)}, u32[]{:S(2)}, u32[]{:S(2)}) async-start(f32[8,16,2048]{2,1,0:T(8,128)} %get-tuple-element.14), calls=%async_computation.3 | async-start | bytes 2097152 | tf_op jit(solution)/shard_map/cond/branch_1_fun/all_to_all | solution.py:314
  102.8 41.8 %collective-permute-start.3 = (f32[128,2048]{1,0:T(8,128)S(1)}, f32[128,2048]{1,0:T(8,128)}, u32[]{:S(2)}, u32[]{:S(2)}) collective-permute-start(f32[128,2048]{1,0:T(8,128)S(1)} %bitcast.20), channel_id=1, source_target_pairs={{0,2},{1,3},{2,0},{3,1},{4,6},{5,7},{6,4},{7,5},{8,10},{9,11},{10,... | collective-permute-start | bytes 3145736 | tf_op jit(solution)/shard_map/cond/branch_1_fun/ppermute | solution.py:17
  127.9 23.1 %collective-permute-start.2 = (f32[128,2048]{1,0:T(8,128)}, f32[128,2048]{1,0:T(8,128)}, u32[]{:S(2)}, u32[]{:S(2)}) collective-permute-start(f32[128,2048]{1,0:T(8,128)} %bitcast.6.mine_ref), channel_id=1, source_target_pairs={{0,2},{1,3},{2,0},{3,1},{4,6},{5,7},{6,4},{7,5},{8,10},{9,11},{10,... | collective-permute-start | bytes 3145736 | tf_op jit(solution)/shard_map/cond/branch_1_fun/ppermute | solution.py:17
  155.8 5.7 %collective-permute-start.5 = (f32[264,128]{1,0:T(8,128)}, f32[264,128]{1,0:T(8,128)S(1)}, u32[]{:S(2)}, u32[]{:S(2)}) collective-permute-start(f32[264,128]{1,0:T(8,128)} %get-tuple-element.33), channel_id=1, source_target_pairs={{0,4},{4,0},{8,12},{12,8},{16,20},{20,16},{24,28},{28,24},{1,5},{5... | collective-permute-start | bytes 405512 | tf_op jit(solution)/shard_map/ppermute | solution.py:257
  162.5 6.0 %collective-permute-start.6 = (f32[264,128]{1,0:T(8,128)S(1)}, f32[264,128]{1,0:T(8,128)S(1)}, u32[]{:S(2)}, u32[]{:S(2)}) collective-permute-start(f32[264,128]{1,0:T(8,128)S(1)} %add.12), channel_id=1, source_target_pairs={{0,8},{4,12},{8,0},{12,4},{16,24},{20,28},{24,16},{28,20},{1,9},{5... | collective-permute-start | bytes 405512 | tf_op jit(solution)/shard_map/ppermute | solution.py:257
  168.5 6.4 %collective-permute-start.7 = (f32[264,128]{1,0:T(8,128)S(1)}, f32[264,128]{1,0:T(8,128)S(1)}, u32[]{:S(2)}, u32[]{:S(2)}) collective-permute-start(f32[264,128]{1,0:T(8,128)S(1)} %add.13), channel_id=1, source_target_pairs={{0,16},{4,20},{8,24},{12,28},{16,0},{20,4},{24,8},{28,12},{1,17},{... | collective-permute-start | bytes 405512 | tf_op jit(solution)/shard_map/ppermute | solution.py:257
